TPU v7x, 256 devices: a whole 4x4x8 slice. The times are simulated.
256 devices in a mesh: var: 8 (over y, core), tok: 32 (over x, z).
Axes of the slice: x: 4, y: 4, z: 8, core: 2. Of those that a mesh axis runs over, the one named last changes fastest.
Arguments:
- patches: bfloat16 [72, 4, 4096], P('var', None, 'tok'), may hold values from -6 to 6
- slot_var: int32 [72], replicated, may hold values from -1 to 47, as said below
- patch_weight: bfloat16 [48, 4, 1024], replicated, may hold values from -3 to 3
- var_embed: bfloat16 [48, 1024], replicated, may hold values from -6 to 6
- query: bfloat16 [1024], replicated, may hold values from -16 to 16
- key_weight: bfloat16 [1024, 1024], P('tok'), may hold values from -0.1875 to 0.1875
- value_weight: bfloat16 [1024, 1024], P('tok'), may hold values from -0.1875 to 0.1875
- out_weight: bfloat16 [1024, 1024], P('tok'), may hold values from -0.1875 to 0.1875
- cotangent: bfloat16 [4096, 1024], P(('tok', 'var')), may hold values from -6 to 6
Outputs:
- aggregated: bfloat16 [4096, 1024], P(('tok', 'var'))
- patch_grad: float32 [72, 4096], P('var', 'tok')
Inputs may be any that keep to these rules, and one draw needn't show every extreme that they name: `slot_var`: slot 9 * i + j belongs to index i of var. Every variable id stands in exactly one slot; empty slots hold -1. The live slots of an index come first and hold consecutive ids, rising from index to index. Every index holds at least one and at most 9 live slots, and some index holds exactly 9.
All inputs are finite; a program needn't handle non-finite values.
Results may differ from a plain program's by a relative error of at most 0.011.
Values may be sent and summed in bfloat16 or wider, within the bound.
No kernel may reach another device: no remote copies, remote signals or barrier semaphores. Data moves between devices by JAX's collectives and lax.ppermute only.
A program may use at most 128 MiB of HBM per device.

v0:
```python
import math

import jax
import jax.numpy as jnp
from jax import lax
from jax.sharding import PartitionSpec as P

H = 16
HD = 64


score_cap = 5.0
inv_sqrt_two = 1.0 / math.sqrt(2.0)
inv_sqrt_two_pi = 1.0 / math.sqrt(2.0 * math.pi)


def gelu_exact(inputs):
    return 0.5 * inputs * (1.0 + lax.erf(inputs * inv_sqrt_two))


def gelu_slope(inputs):
    return (
        0.5 * (1.0 + lax.erf(inputs * inv_sqrt_two))
        + inputs * jnp.exp(-0.5 * inputs * inputs) * inv_sqrt_two_pi
    )


def live_index(slot_var, var_total):
    ids = jnp.arange(var_total, dtype=jnp.int32)
    places = jnp.arange(slot_var.shape[0], dtype=jnp.int32)
    match = slot_var[None, :] == ids[:, None]
    return jnp.sum(jnp.where(match, places[None, :], 0), axis=1)


def attend(embedded, query, key_matrix, value_matrix, out_matrix, cot_rows):
    var_count, tok_count, width = embedded.shape
    flat_rows = embedded.reshape(var_count * tok_count, width)
    key_heads = (
        jnp.dot(flat_rows, key_matrix, preferred_element_type=jnp.float32)
        .astype(jnp.bfloat16)
        .reshape(var_count, tok_count, H, HD)
    )
    value_heads = (
        jnp.dot(flat_rows, value_matrix, preferred_element_type=jnp.float32)
        .astype(jnp.bfloat16)
        .reshape(var_count, tok_count, H, HD)
    )
    query_heads = query.reshape(H, HD)
    raw_scores = jnp.einsum(
        "vthj,hj->tvh", key_heads, query_heads, preferred_element_type=jnp.float32
    ) / math.sqrt(HD)
    squashed = jnp.tanh(raw_scores / score_cap)
    exp_scores = jnp.exp(score_cap * squashed)
    attn_f32 = exp_scores / jnp.sum(exp_scores, axis=1, keepdims=True)
    attn_bf = attn_f32.astype(jnp.bfloat16)
    pooled = (
        jnp.einsum("tvh,vthj->thj", attn_bf, value_heads, preferred_element_type=jnp.float32)
        .astype(jnp.bfloat16)
        .reshape(tok_count, width)
    )
    mixed_out = jnp.dot(pooled, out_matrix, preferred_element_type=jnp.float32).astype(jnp.bfloat16)
    contract = (((1,), (1,)), ((), ()))
    grad_pooled = (
        lax.dot_general(cot_rows, out_matrix, contract, preferred_element_type=jnp.float32)
        .astype(jnp.bfloat16)
        .reshape(tok_count, H, HD)
    )
    grad_attn = jnp.einsum(
        "thj,vthj->tvh", grad_pooled, value_heads, preferred_element_type=jnp.float32
    )
    attn_vth = jnp.transpose(attn_bf, (1, 0, 2)).astype(jnp.float32)
    grad_values = (attn_vth[:, :, :, None] * grad_pooled.astype(jnp.float32)[None]).astype(
        jnp.bfloat16
    )
    grad_scores = attn_f32 * (grad_attn - jnp.sum(attn_f32 * grad_attn, axis=1, keepdims=True))
    grad_raw = grad_scores * (1.0 - squashed * squashed) / math.sqrt(HD)
    query_f32 = query_heads.astype(jnp.float32)
    grad_keys = (jnp.transpose(grad_raw, (1, 0, 2))[:, :, :, None] * query_f32[None, None]).astype(
        jnp.bfloat16
    )
    grad_embed = lax.dot_general(
        grad_keys.reshape(var_count * tok_count, width),
        key_matrix,
        contract,
        preferred_element_type=jnp.float32,
    )
    grad_embed = grad_embed + lax.dot_general(
        grad_values.reshape(var_count * tok_count, width),
        value_matrix,
        contract,
        preferred_element_type=jnp.float32,
    )
    return (mixed_out, grad_embed.astype(jnp.bfloat16).reshape(var_count, tok_count, width))


def body(
    patches,
    slot_var,
    patch_weight,
    var_embed,
    query,
    key_weight,
    value_weight,
    out_weight,
    cotangent,
):
    var_total, _, width = patch_weight.shape
    local_slots = patches.shape[0]
    live_slot = live_index(slot_var, var_total)
    key_matrix, value_matrix = (
        lax.all_gather(key_weight, "tok", axis=0, tiled=True),
        lax.all_gather(value_weight, "tok", axis=0, tiled=True),
    )
    out_matrix = lax.all_gather(out_weight, "tok", axis=0, tiled=True)
    first_slot = lax.axis_index("var") * local_slots
    own_vars = lax.dynamic_slice_in_dim(slot_var, first_slot, local_slots)
    picker = (own_vars[:, None] == jnp.arange(var_total, dtype=jnp.int32)[None, :]).astype(
        jnp.bfloat16
    )
    slot_table = (
        jnp.dot(
            picker, patch_weight.reshape(var_total, 4 * width), preferred_element_type=jnp.float32
        )
        .astype(jnp.bfloat16)
        .reshape(local_slots, 4, width)
    )
    slot_shift = jnp.dot(picker, var_embed, preferred_element_type=jnp.float32)
    pre_act = (
        jnp.einsum("spt,spd->std", patches, slot_table, preferred_element_type=jnp.float32)
        + slot_shift[:, None, :]
    )
    embedded = gelu_exact(pre_act).astype(jnp.bfloat16)
    spread = lax.all_to_all(embedded, "var", split_axis=1, concat_axis=0, tiled=True)
    live_rows = jnp.take(spread, live_slot, axis=0)
    mixed_out, grad_embed = attend(
        live_rows, query, key_matrix, value_matrix, out_matrix, cotangent
    )
    grad_slots = jnp.zeros(spread.shape, jnp.bfloat16).at[live_slot].set(grad_embed)
    returned = lax.all_to_all(grad_slots, "var", split_axis=0, concat_axis=1, tiled=True)
    grad_pre = returned.astype(jnp.float32) * gelu_slope(pre_act)
    slot_grad = jnp.einsum(
        "spt,std->spd", patches.astype(jnp.float32), grad_pre, precision=lax.Precision.HIGHEST
    ).reshape(local_slots, 4 * width)
    grad_out = lax.psum_scatter(slot_grad, "tok", scatter_dimension=1, tiled=True)
    return (mixed_out, grad_out)


def solution(mesh):
    return jax.shard_map(
        body,
        mesh=mesh,
        in_specs=(
            P("var", None, "tok"),
            P(),
            P(),
            P(),
            P(),
            P("tok", None),
            P("tok", None),
            P("tok", None),
            P(("tok", "var"), None),
        ),
        out_specs=(P(("tok", "var"), None), P("var", "tok")),
        check_vma=False,
    )
```

profile of v0, /device:TPU:32, one launch (start us, length us, event | category | flops | bytes accessed | tf_op | source)
XLA Modules:
  0.0 544.2 jit_solution(2519850298434397522)
XLA Ops:
  7.2 0.7 all-gather.8.cloned.1.call-update
  8.0 0.7 all-gather.6.cloned.1.call-update
  8.7 0.7 all-gather.4.cloned.1.call-update
  9.4 1.1 copy.47
  10.5 0.7 dynamic_slice.3
  11.3 0.2 convolution_convert_fusion
  11.6 0.2 fusion.30
  11.8 4.6 fusion.6
  16.3 6.6 %copy.29 = bf16[9,128,1024]{2,0,1:T(8,128)(2,1)} copy(bf16[9,128,1024]{1,2,0:T(8,128)(2,1)S(1)} %get-tuple-element.6) | data formatting | bytes 4718592 | tf_op jit(solution)/shard_map/convert_element_type | solution.py:132
  22.9 4.7 all-to-all-start
  28.1 49.2 %all-to-all-done = bf16[9,128,1024]{2,0,1:T(8,128)(2,1)} async-done(((bf16[9,128,1024]{2,0,1:T(8,128)(2,1)}), bf16[9,128,1024]{2,0,1:T(8,128)(2,1)}, u32[]{:S(2)}, u32[]{:S(2)}) %all-to-all-start) | async-done | bytes 2359328 | tf_op jit(solution)/shard_map/all_to_all | solution.py:133
  77.3 3.8 copy.31
  81.0 1.9 gather_fusion
  82.9 1.6 bitcast_select_fusion
  84.5 5.4 all-gather.8.cloned.1.call-done
  90.0 2.2 convolution_convert_fusion.3
  92.2 0.1 reshape.117
  92.5 75.3 %all-gather.6.cloned.1.call-done = bf16[1024,1024]{1,0:T(8,128)(2,1)} async-done(((bf16[32,1024]{1,0:T(8,128)(2,1)}), bf16[1024,1024]{1,0:T(8,128)(2,1)}) %all-gather.6.cloned.1.call-update) | async-done | bytes 2097168 | tf_op jit(solution)/shard_map/all_gather | solution.py:112
  167.8 4.6 convolution_convert_fusion.1
  172.4 4.1 reshape.85
  176.5 69.0 %all-gather.4.cloned.1.call-done = bf16[1024,1024]{1,0:T(8,128)(2,1)} async-done(((bf16[32,1024]{1,0:T(8,128)(2,1)}), bf16[1024,1024]{1,0:T(8,128)(2,1)}) %all-gather.4.cloned.1.call-update) | async-done | bytes 2097168 | tf_op jit(solution)/shard_map/all_gather | solution.py:111
  245.6 5.0 convolution_convert_fusion.2
  250.6 5.2 reshape.83
  255.8 5.3 fusion.12
  261.2 0.2 bitcast_reduce_fusion
  261.3 1.9 fusion.14
  263.3 0.2 multiply_reduce_fusion
  263.5 0.1 convert_convert_fusion
  263.6 0.2 copy.32
  263.9 3.8 mul.100
  267.7 6.3 %mul.101 = f32[768,1024]{1,0:T(8,128)} reshape(f32[48,16,16,64]{3,2,1,0:T(8,128)} %mul.100) | data formatting | bytes 6291456 | tf_op jit(solution)/shard_map/mul | solution.py:78
  274.0 1.0 copy.33
  275.0 3.3 multiply_convert_fusion
  278.3 3.2 convert_element_type.86
  281.5 4.5 fusion.22
  286.0 3.0 add_convert_fusion
  289.0 0.3 broadcast_in_dim.48
  289.3 5.1 scatter_fusion
  294.4 34.1 %all_to_all.27 = bf16[72,16,1024]{2,1,0:T(8,128)(2,1)S(1)} all-to-all(bf16[72,16,1024]{2,1,0:T(8,128)(2,1)S(1)} %scatter_fusion), channel_id=1, replica_groups=mesh['var'=8,'tok'=32] {'var'}, dimensions={0} | all-to-all | bytes 4718592 | tf_op jit(solution)/shard_map/all_to_all | solution.py:139
  328.5 0.6 convert_bitcast_fusion
  329.1 2.8 copy.34
  332.0 6.0 %copy.35 = f32[9,128,1024]{1,2,0:T(8,128)} copy(f32[9,128,1024]{2,1,0:T(8,128)} %bitcast.116) | data formatting | bytes 9437184 | tf_op jit(solution)/shard_map/convert_element_type | solution.py:140
  338.0 6.8 %fusion.24 = f32[9,4,1024]{2,1,0:T(4,128)S(1)} fusion(bf16[9,4,128]{2,1,0:T(4,128)(2,1)S(1)} %copy-done.7, f32[9,128,1024]{1,2,0:T(8,128)} %copy.35, f32[9,1024,128]{2,1,0:T(8,128)} %get-tuple-element.7, f32[9,1024]{1,0:T(8,128)S(1)} %fusion.30), kind=kOutput, calls=%fused_computation.36 | convolution fusion | flops 68419584 | bytes 9630720 | tf_op jit(solution)/shard_map/spt,std->spd/dot_general | solution.py:141
  344.9 0.9 copy.48
  345.8 3.8 fusion.16
  349.6 0.1 reshape.86
  349.7 1.0 convolution_convert_fusion.4
  350.8 186.9 %reduce-scatter.2.cloned.1.call-done = f32[9,128]{1,0:T(8,128)} async-done(((f32[9,4096]{1,0:T(8,128)}), f32[9,128]{1,0:T(8,128)}) %reduce-scatter.2.cloned.1.call-update) | async-done | bytes 4624 | tf_op jit(solution)/shard_map/reduce_scatter | solution.py:144
  (40 shorter events, 0.8 us)
Async XLA Ops:
  7.2 4.4 copy-start
  7.2 82.8 %all-gather.8.cloned.1.call-start = ((), (), s32[]{:S(2)}) async-start(), calls=%async_computation.5 | async-start | bytes 2162688 | tf_op jit(solution)/shard_map/all_gather | solution.py:114
  7.9 159.9 %all-gather.6.cloned.1.call-start = ((), (), s32[]{:S(2)}) async-start(), calls=%async_computation.4 | async-start | bytes 2162688 | tf_op jit(solution)/shard_map/all_gather | solution.py:112
  8.7 236.9 %all-gather.4.cloned.1.call-start = ((), (), s32[]{:S(2)}) async-start(), calls=%async_computation.3 | async-start | bytes 2162688 | tf_op jit(solution)/shard_map/all_gather | solution.py:111
  22.9 4.8 copy-start.8
  22.9 4.8 copy-start.10
  22.9 54.3 %all-to-all-start = ((bf16[9,128,1024]{2,0,1:T(8,128)(2,1)}), bf16[9,128,1024]{2,0,1:T(8,128)(2,1)}, u32[]{:S(2)}, u32[]{:S(2)}) async-start(bf16[9,128,1024]{2,0,1:T(8,128)(2,1)} %copy.29), calls=%async_computation | async-start | bytes 8388608 | tf_op jit(solution)/shard_map/all_to_all | solution.py:133
  27.6 510.0 %reduce-scatter.2.cloned.1.call-start = ((), (), s32[]{:S(2)}) async-start(), calls=%async_computation.6 | async-start | bytes 270336 | tf_op jit(solution)/shard_map/reduce_scatter | solution.py:144
  81.0 9.0 %copy-start.6 = (bf16[16,1024]{1,0:T(8,128)(2,1)S(1)}, bf16[16,1024]{1,0:T(8,128)(2,1)}, u32[]{:S(2)}) copy-start(bf16[16,1024]{1,0:T(8,128)(2,1)} %param.17) | copy-start | bytes 98308
  84.5 83.3 %copy-start.4 = (bf16[768,1024]{1,0:T(8,128)(2,1)}, bf16[768,1024]{1,0:T(8,128)(2,1)S(1)}, u32[]{:S(2)}) copy-start(bf16[768,1024]{1,0:T(8,128)(2,1)S(1)} %bitcast_select_fusion) | copy-start | bytes 4718596
  176.5 84.8 %copy-start.3 = (bf16[48,16,16,64]{3,2,1,0:T(8,128)(2,1)}, bf16[48,16,16,64]{3,2,1,0:T(8,128)(2,1)S(1)}, u32[]{:S(2)}) copy-start(bf16[48,16,16,64]{3,2,1,0:T(8,128)(2,1)S(1)} %reshape.85) | copy-start | bytes 4718596
  281.5 4.5 copy-start.5
  281.5 4.5 copy-start.9
  332.0 6.1 %copy-start.7 = (bf16[9,4,128]{2,1,0:T(4,128)(2,1)S(1)}, bf16[9,4,128]{2,1,0:T(4,128)(2,1)}, u32[]{:S(2)}) copy-start(bf16[9,4,128]{2,1,0:T(4,128)(2,1)} %param.9) | copy-start | bytes 27652
  344.9 4.9 copy-start.2
  345.8 191.8 %copy-start.1 = (bf16[48,1024]{1,0:T(8,128)(2,1)S(1)}, bf16[48,1024]{1,0:T(8,128)(2,1)}, u32[]{:S(2)}) copy-start(bf16[48,1024]{1,0:T(8,128)(2,1)} %param.12) | copy-start | bytes 294916
Sparse Core Ops, SparseCore 0:
  10.6 79.3 all-gather.7
  92.6 75.2 all-gather.5
  170.4 75.0 all-gather.3
  345.9 191.6 reduce-scatter.1
where the time goes:
time: 546 us; the launch traced here: 544 us
  waiting for transfers between devices  388 us (71%)
  local copies, waits for them, and re-layouts  53.8 us (10%)
  matrix products  43.2 us (8%)
  blocking collectives  34.1 us (6%)
  between operations  14.1 us (3%)
  other arithmetic  6.16 us (1%)
    reduce_scatter x1, waiting for transfers between devices, body(): lax.psum_scatter(slot_grad, 'tok', scatter_dimension=1, tiled=True)  187 us
    all_gather x1, waiting for transfers between devices, body(): lax.all_gather(value_weight, 'tok', axis=0, tiled=True)  75.3 us
    all_gather x1, waiting for transfers between devices, body(): lax.all_gather(key_weight, 'tok', axis=0, tiled=True)  69 us
    all_to_all x1, waiting for transfers between devices, body(): lax.all_to_all(embedded, 'var', split_axis=1, concat_axis=0, tiled=True)  49.2 us
    all_to_all x1, blocking collectives, body(): lax.all_to_all(grad_slots, 'var', split_axis=0, concat_axis=1, tiled=True)  34.1 us
  transfers between devices with their start and end apart: 5, of which 5 were waited for; matrix products, arithmetic and copies ran while one was open for 7% of the time, Pallas kernels for 0%

commit v1 on v0

v1 whole, which is shorter than its diff:
```python
import math

import jax
import jax.numpy as jnp
from jax import lax
from jax.sharding import PartitionSpec as P

H = 16
HD = 64


score_cap = 5.0
inv_sqrt_two = 1.0 / math.sqrt(2.0)
inv_sqrt_two_pi = 1.0 / math.sqrt(2.0 * math.pi)

f32 = jnp.float32
bf16 = jnp.bfloat16


def gelu_exact(inputs):
    return 0.5 * inputs * (1.0 + lax.erf(inputs * inv_sqrt_two))


def gelu_slope(inputs):
    return (
        0.5 * (1.0 + lax.erf(inputs * inv_sqrt_two))
        + inputs * jnp.exp(-0.5 * inputs * inputs) * inv_sqrt_two_pi
    )


def live_index(slot_var, var_total):
    ids = jnp.arange(var_total, dtype=jnp.int32)
    places = jnp.arange(slot_var.shape[0], dtype=jnp.int32)
    match = slot_var[None, :] == ids[:, None]
    return jnp.sum(jnp.where(match, places[None, :], 0), axis=1)


def split(x):
    hi = x.astype(bf16)
    lo = (x - hi.astype(f32)).astype(bf16)
    return hi, lo


def ein(spec, a, b):
    return jnp.einsum(spec, a, b, preferred_element_type=f32)


def body(
    patches,
    slot_var,
    patch_weight,
    var_embed,
    query,
    key_weight,
    value_weight,
    out_weight,
    cotangent,
    *,
    n_var,
    n_tok,
):
    var_total, pixels_per, width = patch_weight.shape
    local_slots = patches.shape[0]
    rows = key_weight.shape[0]
    tok_count = cotangent.shape[0]

    query_heads = query.reshape(H, HD).astype(f32)
    wq_rows = jnp.sum(key_weight.reshape(rows, H, HD).astype(f32) * query_heads[None], axis=2)
    wq_hi, wq_lo = split(wq_rows)
    pad = (-(2 * width + 2 * H)) % 128
    packed = jnp.concatenate(
        [value_weight, out_weight, wq_hi, wq_lo, jnp.zeros((rows, pad), bf16)], axis=1
    )
    full = lax.all_gather(packed, "tok", axis=0, tiled=True)
    value_matrix = full[:, :width]
    out_matrix = full[:, width : 2 * width]
    wq_hi = full[:, 2 * width : 2 * width + H]
    wq_lo = full[:, 2 * width + H : 2 * width + 2 * H]

    slot_pixels = lax.all_to_all(patches, "var", 2, 0, tiled=True)
    live_slot = live_index(slot_var, var_total)
    pixels = jnp.take(slot_pixels, live_slot, axis=0)
    pre_act = ein("vpt,vpd->vtd", pixels, patch_weight) + var_embed.astype(f32)[:, None, :]
    embedded = gelu_exact(pre_act).astype(bf16)

    raw_scores = (ein("vtd,dh->tvh", embedded, wq_hi) + ein("vtd,dh->tvh", embedded, wq_lo)) / math.sqrt(HD)
    squashed = jnp.tanh(raw_scores / score_cap)
    exp_scores = jnp.exp(score_cap * squashed)
    attn_f32 = exp_scores / jnp.sum(exp_scores, axis=1, keepdims=True)
    attn_bf = attn_f32.astype(bf16)

    value_heads = value_matrix.reshape(width, H, HD)
    mixed_in = ein("tvh,vtd->thd", attn_bf, embedded)
    mix_hi, mix_lo = split(mixed_in)
    pooled = (
        (ein("thd,dhj->thj", mix_hi, value_heads) + ein("thd,dhj->thj", mix_lo, value_heads))
        .astype(bf16)
        .reshape(tok_count, width)
    )
    mixed_out = jnp.dot(pooled, out_matrix, preferred_element_type=f32).astype(bf16)
    contract = (((1,), (1,)), ((), ()))
    grad_pooled = (
        lax.dot_general(cotangent, out_matrix, contract, preferred_element_type=f32)
        .astype(bf16)
        .reshape(tok_count, H, HD)
    )
    spread = ein("thj,dhj->thd", grad_pooled, value_heads)
    spread_hi, spread_lo = split(spread)
    grad_attn = ein("vtd,thd->tvh", embedded, spread_hi) + ein("vtd,thd->tvh", embedded, spread_lo)
    grad_scores = attn_f32 * (grad_attn - jnp.sum(attn_f32 * grad_attn, axis=1, keepdims=True))
    grad_raw = grad_scores * (1.0 - squashed * squashed) / math.sqrt(HD)
    raw_hi, raw_lo = split(grad_raw)
    grad_embed = (
        ein("tvh,thd->vtd", attn_bf, spread_hi)
        + ein("tvh,thd->vtd", attn_bf, spread_lo)
        + ein("tvh,dh->vtd", raw_hi, wq_hi)
        + ein("tvh,dh->vtd", raw_hi, wq_lo)
        + ein("tvh,dh->vtd", raw_lo, wq_hi)
    ).astype(bf16)
    grad_pre = grad_embed.astype(f32) * gelu_slope(pre_act)
    partial = jnp.einsum(
        "vpt,vtd->vpd", pixels.astype(f32), grad_pre, precision=lax.Precision.HIGHEST
    ).reshape(var_total, pixels_per * width)

    slots = n_var * local_slots
    cols = partial.shape[1] // n_tok
    safe = jnp.clip(slot_var, 0, var_total - 1)
    slot_rows = jnp.where((slot_var >= 0)[:, None], jnp.take(partial, safe, axis=0), 0.0)
    blocks = slot_rows.reshape(n_var, local_slots, n_tok, cols).transpose(0, 2, 1, 3)
    by_var = lax.all_to_all(blocks, "var", 0, 0, tiled=True).sum(axis=0)
    by_tok = lax.all_to_all(by_var, "tok", 0, 0, tiled=True).sum(axis=0)
    del slots
    return (mixed_out, by_tok)


def solution(mesh):
    import functools

    fn = functools.partial(body, n_var=mesh.shape["var"], n_tok=mesh.shape["tok"])
    return jax.shard_map(
        fn,
        mesh=mesh,
        in_specs=(
            P("var", None, "tok"),
            P(),
            P(),
            P(),
            P(),
            P("tok", None),
            P("tok", None),
            P("tok", None),
            P(("tok", "var"), None),
        ),
        out_specs=(P(("tok", "var"), None), P("var", "tok")),
        check_vma=False,
    )
```

time: 546 us -> 187 us (0.34)
  waiting for transfers between devices: 388 us -> 93.8 us
  local copies, waits for them, and re-layouts: 53.8 us -> 19.2 us
  blocking collectives: 34.1 us -> 0 us
  starting transfers between devices: 4.84 us -> 14.7 us
  matrix products: 43.2 us -> 37 us
    reduce_scatter x1 -> x0, waiting for transfers between devices: 187 us -> none  [body(): lax.psum_scatter(slot_grad, 'tok', scatter_dimension=1, tiled=True)]
    all_gather x3 -> x1, waiting for transfers between devices: 150 us -> 68.8 us  [body(): full = lax.all_gather(packed, 'tok', axis=0, tiled=True)]
    all_to_all x1 -> x0, blocking collectives: 34.1 us -> none  [body(): lax.all_to_all(grad_slots, 'var', split_axis=0, concat_axis=1, tiled=True)]
    all_to_all x1 -> x3, waiting for transfers between devices: 49.2 us -> 25 us  [the longest x1 13.6 us: body(): by_var = lax.all_to_all(blocks, 'var', 0, 0, tiled=True).sum(axis=0)]
    convert_element_type x5, local copies, waits for them, and re-layouts: 19.6 us -> 2.22 us  [the longest x1 1.01 us: body(): key_weight.reshape(rows, H, HD).astype(f32) * query_heads[None]]
    mul x2 -> x0, local copies, waits for them, and re-layouts: 10.1 us -> none  [attend(): jnp.transpose(grad_raw, (1, 0, 2))[:, :, :, None] * query_f32[None, None]]
    all_to_all x1 -> x3, starting transfers between devices: 4.69 us -> 14.7 us  [the longest x1 5.9 us: body(): by_tok = lax.all_to_all(by_var, 'tok', 0, 0, tiled=True).sum(axis=0)]
    reshape x7 -> x2, local copies, waits for them, and re-layouts: 9.87 us -> 0.24 us  [the longest x1 0.13 us: body(): grad_pooled = lax.dot_general(cotangent, out_matrix, contract, preferred_...]
  transfers between devices with their start and end apart: 5 -> 4, of which waited for: 5 -> 4; matrix products, arithmetic and copies ran while one was open for 7% -> 9% of each run, Pallas kernels for 0% -> 0%
where the time goes in v1:
time: 187 us; the launch traced here: 186 us
  waiting for transfers between devices  93.8 us (50%)
  matrix products  37 us (20%)
  local copies, waits for them, and re-layouts  19.2 us (10%)
  starting transfers between devices  14.7 us (8%)
  between operations  14.3 us (8%)
  other arithmetic  7.18 us (4%)
    all_gather x1, waiting for transfers between devices, body(): full = lax.all_gather(packed, 'tok', axis=0, tiled=True)  68.8 us
    dot_general x14, matrix products, ein(): return jnp.einsum(spec, a, b, preferred_element_type=f32)  29.2 us
    all_to_all x1, waiting for transfers between devices, body(): by_var = lax.all_to_all(blocks, 'var', 0, 0, tiled=True).sum(axis=0)  13.6 us
    all_to_all x1, waiting for transfers between devices, body(): by_tok = lax.all_to_all(by_var, 'tok', 0, 0, tiled=True).sum(axis=0)  8.57 us
    slice x2, local copies, waits for them, and re-layouts, body(): value_matrix = full[:, :width]  6.2 us
    all_to_all x1, starting transfers between devices, body(): by_tok = lax.all_to_all(by_var, 'tok', 0, 0, tiled=True).sum(axis=0)  5.9 us
    unnamed x17, local copies, waits for them, and re-layouts  4.92 us
    all_to_all x1, starting transfers between devices, body(): slot_pixels = lax.all_to_all(patches, 'var', 2, 0, tiled=True)  4.47 us
  transfers between devices with their start and end apart: 4, of which 4 were waited for; matrix products, arithmetic and copies ran while one was open for 9% of the time, Pallas kernels for 0%

profile of v1, /device:TPU:32, one launch (start us, length us, event | category | flops | bytes accessed | tf_op | source)
XLA Modules:
  0.0 186.2 jit_solution(18231606035515300481)
XLA Ops:
  7.2 1.0 reshape.71
  8.2 0.8 reshape.72
  9.2 1.6 concatenate.3
  10.8 0.9 copy.112
  11.7 0.8 reshape.92
  12.4 4.5 %all-to-all-start = ((bf16[8,2,288]{2,1,0:T(2,128)(2,1)}), bf16[8,2,288]{2,1,0:T(2,128)(2,1)S(1)}, u32[]{:S(2)}, u32[]{:S(2)}) async-start(bf16[8,2,288]{2,1,0:T(2,128)(2,1)} %reshape.92), calls=%async_computation | async-start | bytes 24576 | tf_op jit(solution)/shard_map/all_to_all | solution.py:80
  16.9 0.8 select_reduce_fusion
  17.7 0.7 compare_and_fusion
  18.4 0.9 convert_element_type.90
  19.5 2.8 %all-to-all-done = bf16[8,2,288]{2,1,0:T(2,128)(2,1)S(1)} async-done(((bf16[8,2,288]{2,1,0:T(2,128)(2,1)}), bf16[8,2,288]{2,1,0:T(2,128)(2,1)S(1)}, u32[]{:S(2)}, u32[]{:S(2)}) %all-to-all-start) | async-done | bytes 9248 | tf_op jit(solution)/shard_map/all_to_all | solution.py:80
  22.3 0.3 reshape.93
  22.7 0.3 copy.135
  23.0 0.6 gather_fusion
  23.6 3.2 %multiply_convert_fusion = (bf16[48,16,1024]{2,1,0:T(8,128)(2,1)}, f32[48,16,1024]{2,1,0:T(8,128)}) fusion(f32[48,1024]{1,0:T(8,128)S(1)} %convert_element_type.90, bf16[48,4,1024]{2,1,0:T(4,128)(2,1)S(1)} %copy-done, bf16[48,4,16]{2,1,0:T(4,128)(2,1)S(1)} %gather_fusion, pred[48]{0:T(512)(128)(4,1)S(1)} %compare_and_fusion.1), kind=kOutput, calls=%fused_computation.17 | convolution fusion | flops 11013120 | bytes 5314608 | tf_op jit(solution)/shard_map/vpt,vpd->vtd/dot_general | solution.py:45
  26.8 68.8 %all-gather.2.cloned.1.call-done = bf16[1024,2176]{1,0:T(8,128)(2,1)} async-done(((bf16[32,2176]{1,0:T(8,128)(2,1)}), bf16[1024,2176]{1,0:T(8,128)(2,1)}) %all-gather.2.cloned.1.call-update) | async-done | bytes 4456464 | tf_op jit(solution)/shard_map/all_gather | solution.py:74
  95.6 3.2 %slice.20 = bf16[1024,1024]{1,0:T(8,128)(2,1)} slice(bf16[1024,2176]{1,0:T(8,128)(2,1)} %all-gather.2.cloned.1.call-done), slice={[0:1024], [0:1024]} | slice | bytes 4194304 | tf_op jit(solution)/shard_map/slice | solution.py:75
  98.8 3.0 %copy.110 = bf16[1024,1024]{0,1:T(8,128)(2,1)S(1)} copy(bf16[1024,1024]{1,0:T(8,128)(2,1)} %slice.20) | data formatting | bytes 4194304 | tf_op jit(solution)/shard_map/slice | solution.py:75
  101.8 2.2 %fusion.34 = bf16[16,1024]{1,0:T(8,128)(2,1)S(1)} fusion(bf16[16,1024]{1,0:T(8,128)(2,1)S(1)} %copy-done.5, bf16[1024,2176]{1,0:T(8,128)(2,1)} %all-gather.2.cloned.1.call-done), kind=kOutput, calls=%fused_computation.43 | convolution fusion | flops 33570816 | bytes 2162688 | tf_op jit(solution)/shard_map/dot_general | solution.py:103
  104.2 0.4 subtract_convert_fusion
  104.6 1.0 copy-done.3
  105.6 1.2 fusion.38
  106.8 2.1 %fusion.43 = f32[16,48,16]{1,0,2:T(8,128)S(1)} fusion(bf16[48,16,1024]{2,1,0:T(8,128)(2,1)S(1)} %copy-done.3, bf16[1024,2176]{1,0:T(8,128)(2,1)} %all-gather.2.cloned.1.call-done), kind=kOutput, calls=%fused_computation.52 | convolution fusion | flops 25165824 | bytes 1884160 | tf_op jit(solution)/shard_map/vtd,dh->tvh/dot_general | solution.py:45
  108.9 2.4 %bitcast_reduce_fusion = (f32[16,16]{1,0:T(8,128)S(1)}, f32[16,48,16]{1,0,2:T(8,128)S(1)}) fusion(f32[16,48,16]{1,0,2:T(8,128)S(1)} %fusion.43, bf16[48,16,1024]{2,1,0:T(8,128)(2,1)S(1)} %copy-done.3, bf16[1024,2176]{1,0:T(8,128)(2,1)} %all-gather.2.cloned.1.call-done), kind=kOutput, calls=%fused_computation.69 | convolution fusion | flops 25214720 | bytes 1934336 | tf_op jit(solution)/shard_map/vtd,dh->tvh/dot_general | solution.py:45
  111.4 2.4 %fusion.52 = f32[16,1024,48]{1,2,0:T(8,128)} fusion(bf16[16,48,16]{1,2,0:T(8,128)(2,1)S(1)} %fusion.58, bf16[16,16,1024]{2,0,1:T(8,128)(2,1)S(1)} %get-tuple-element.11), kind=kOutput, calls=%fused_computation.61 | convolution fusion | flops 25165824 | bytes 3694592 | tf_op jit(solution)/shard_map/tvh,thd->vtd/dot_general | solution.py:45
  113.8 2.3 %fusion.49 = f32[16,1024,48]{1,2,0:T(8,128)} fusion(bf16[16,48,16]{1,2,0:T(8,128)(2,1)S(1)} %fusion.58, bf16[16,16,1024]{2,0,1:T(8,128)(2,1)S(1)} %get-tuple-element.10), kind=kOutput, calls=%fused_computation.58 | convolution fusion | flops 25165824 | bytes 3694592 | tf_op jit(solution)/shard_map/tvh,thd->vtd/dot_general | solution.py:45
  116.2 2.3 %convolution_add_fusion.2 = f32[16,48,16]{1,2,0:T(8,128)S(1)} fusion(f32[16,48,16]{1,2,0:T(8,128)S(1)} %fusion.38, bf16[48,16,1024]{2,1,0:T(8,128)(2,1)S(1)} %copy-done.3, bf16[16,16,1024]{2,0,1:T(8,128)(2,1)S(1)} %get-tuple-element.10), kind=kOutput, calls=%fused_computation.38 | convolution fusion | flops 25178112 | bytes 2195456 | tf_op jit(solution)/shard_map/vtd,thd->tvh/dot_general | solution.py:45
  118.4 1.3 subtract_convert_fusion.2
  119.7 0.2 copy.131
  120.0 0.2 copy.133
  120.2 1.7 fusion.54
  121.9 1.7 fusion.55
  123.7 5.0 %fusion.8 = bf16[48,16,1024]{2,1,0:T(8,128)(2,1)S(1)} fusion(f32[1024,16,48]{0,1,2:T(8,128)S(1)} %fusion.54, f32[1024,16,48]{0,1,2:T(8,128)S(1)} %fusion.55, f32[16,1024,48]{1,2,0:T(8,128)S(1)} %copy-done.2, f32[16,1024,48]{1,2,0:T(8,128)S(1)} %copy-done.1, bf16[16,48,16]{2,0,1:T(8,128)(2,1)S(1)} %copy.133, bf16[1024,2176]{1,0:T(8,128)(2,1)} %all-gather.2.cloned.1.call-done), kind=kOutput, calls=%fused_computation.11 | convolution fusion | flops 29097984 | bytes 14442496 | tf_op jit(solution)/shard_map/tvh,dh->vtd/dot_general | solution.py:45
  128.7 2.9 %fusion.6 = f32[48,4,1024]{2,1,0:T(4,128)S(1)} fusion(bf16[48,16,1024]{2,1,0:T(8,128)(2,1)S(1)} %fusion.8, f32[48,16,1024]{2,1,0:T(8,128)S(1)} %copy-done.4, f32[48,1024]{1,0:T(8,128)S(1)} %convert_element_type.90, bf16[48,4,16]{2,1,0:T(4,128)(2,1)S(1)} %gather_fusion, pred[48]{0:T(512)(128)(4,1)S(1)} %compare_and_fusion.1), kind=kOutput, calls=%fused_computation.9 | convolution fusion | flops 46402560 | bytes 5707824 | tf_op jit(solution)/shard_map/vpt,vtd->vpd/dot_general | solution.py:121
  131.7 0.5 copy.138
  132.1 2.0 %gather_fusion.1 = f32[72,4096]{1,0:T(8,128)} fusion(f32[48,4096]{1,0:T(8,128)S(1)} %bitcast.84, s32[1024]{0:T(1024)S(1)} %pad_clamp_fusion), kind=kCustom, calls=%fused_computation.1 | custom fusion | bytes 2359584 | tf_op jit(solution)/shard_map/jit(_take)/gather | solution.py:128
  134.1 1.5 copy.139
  135.6 1.3 select_bitcast_fusion
  136.9 4.3 %all-to-all-start.1 = ((f32[8,32,9,128]{3,1,2,0:T(8,128)}), f32[8,32,9,128]{3,1,2,0:T(8,128)}, u32[]{:S(2)}, u32[]{:S(2)}) async-start(f32[8,32,9,128]{3,1,2,0:T(8,128)} %select_bitcast_fusion), calls=%async_computation.1 | async-start | bytes 2359296 | tf_op jit(solution)/shard_map/all_to_all | solution.py:130
  141.2 3.2 %subtract_convert_fusion.1 = (bf16[16,16,1024]{2,1,0:T(8,128)(2,1)S(1)}, bf16[16,16,1024]{2,1,0:T(8,128)(2,1)S(1)}) fusion(bf16[16,48,16]{1,2,0:T(8,128)(2,1)S(1)} %fusion.58, bf16[48,16,1024]{2,1,0:T(8,128)(2,1)} %get-tuple-element.13), kind=kOutput, calls=%fused_computation.45 | convolution fusion | flops 26214400 | bytes 2646016 | tf_op jit(solution)/shard_map/tvh,vtd->thd/dot_general | solution.py:45
  144.3 0.6 fusion.46
  145.0 13.6 %all-to-all-done.1 = f32[8,32,9,128]{3,1,2,0:T(8,128)} async-done(((f32[8,32,9,128]{3,1,2,0:T(8,128)}), f32[8,32,9,128]{3,1,2,0:T(8,128)}, u32[]{:S(2)}, u32[]{:S(2)}) %all-to-all-start.1) | async-done | bytes 1179680 | tf_op jit(solution)/shard_map/all_to_all | solution.py:130
  158.6 1.4 reduce_sum.61
  160.0 0.8 copy.134
  160.8 5.9 %all-to-all-start.2 = ((f32[32,9,128]{2,1,0:T(8,128)}), f32[32,9,128]{2,1,0:T(8,128)S(1)}, u32[]{:S(2)}, u32[]{:S(2)}) async-start(f32[32,9,128]{2,1,0:T(8,128)} %copy.134), calls=%async_computation.2 | async-start | bytes 524288 | tf_op jit(solution)/shard_map/all_to_all | solution.py:131
  166.7 0.7 fusion.27
  167.5 2.6 %fusion.28 = bf16[16,1024]{1,0:T(8,128)(2,1)} fusion(bf16[16,1024]{1,0:T(8,128)(2,1)S(1)} %reshape.68, bf16[1024,2176]{1,0:T(8,128)(2,1)} %all-gather.2.cloned.1.call-done), kind=kOutput, calls=%fused_computation.41 | convolution fusion | flops 33570816 | bytes 2162688 | tf_op jit(solution)/shard_map/dot_general | solution.py:100
  170.1 8.6 %all-to-all-done.2 = f32[32,9,128]{2,1,0:T(8,128)S(1)} async-done(((f32[32,9,128]{2,1,0:T(8,128)}), f32[32,9,128]{2,1,0:T(8,128)S(1)}, u32[]{:S(2)}, u32[]{:S(2)}) %all-to-all-start.2) | async-done | bytes 147488 | tf_op jit(solution)/shard_map/all_to_all | solution.py:131
  178.7 0.6 reduce_sum.62
  (27 shorter events, 0.9 us)
Async XLA Ops:
  7.2 16.4 %copy-start = (bf16[48,4,1024]{2,1,0:T(4,128)(2,1)S(1)}, bf16[48,4,1024]{2,1,0:T(4,128)(2,1)}, u32[]{:S(2)}) copy-start(bf16[48,4,1024]{2,1,0:T(4,128)(2,1)} %param.11) | copy-start | bytes 1179652
  7.2 88.4 %all-gather.2.cloned.1.call-start = ((), (), s32[]{:S(2)}) async-start(), calls=%async_computation.3 | async-start | bytes 4595712 | tf_op jit(solution)/shard_map/all_gather | solution.py:74
  12.4 9.8 %all-to-all-start = ((bf16[8,2,288]{2,1,0:T(2,128)(2,1)}), bf16[8,2,288]{2,1,0:T(2,128)(2,1)S(1)}, u32[]{:S(2)}, u32[]{:S(2)}) async-start(bf16[8,2,288]{2,1,0:T(2,128)(2,1)} %reshape.92), calls=%async_computation | async-start | bytes 24576 | tf_op jit(solution)/shard_map/all_to_all | solution.py:80
  26.8 75.1 %copy-start.5 = (bf16[16,1024]{1,0:T(8,128)(2,1)S(1)}, bf16[16,1024]{1,0:T(8,128)(2,1)}, u32[]{:S(2)}) copy-start(bf16[16,1024]{1,0:T(8,128)(2,1)} %param.17) | copy-start | bytes 98308
  104.2 1.4 copy-start.3
  120.2 3.5 %copy-start.1 = (f32[16,1024,48]{1,2,0:T(8,128)S(1)}, f32[16,1024,48]{1,2,0:T(8,128)}, u32[]{:S(2)}) copy-start(f32[16,1024,48]{1,2,0:T(8,128)} %fusion.52) | copy-start | bytes 9437188
  120.2 3.5 %copy-start.2 = (f32[16,1024,48]{1,2,0:T(8,128)S(1)}, f32[16,1024,48]{1,2,0:T(8,128)}, u32[]{:S(2)}) copy-start(f32[16,1024,48]{1,2,0:T(8,128)} %fusion.49) | copy-start | bytes 9437188
  123.6 5.1 %copy-start.4 = (f32[48,16,1024]{2,1,0:T(8,128)S(1)}, f32[48,16,1024]{2,1,0:T(8,128)}, u32[]{:S(2)}) copy-start(f32[48,16,1024]{2,1,0:T(8,128)} %get-tuple-element.14) | copy-start | bytes 9437188
  136.9 21.8 %all-to-all-start.1 = ((f32[8,32,9,128]{3,1,2,0:T(8,128)}), f32[8,32,9,128]{3,1,2,0:T(8,128)}, u32[]{:S(2)}, u32[]{:S(2)}) async-start(f32[8,32,9,128]{3,1,2,0:T(8,128)} %select_bitcast_fusion), calls=%async_computation.1 | async-start | bytes 2359296 | tf_op jit(solution)/shard_map/all_to_all | solution.py:130
  160.8 17.9 %all-to-all-start.2 = ((f32[32,9,128]{2,1,0:T(8,128)}), f32[32,9,128]{2,1,0:T(8,128)S(1)}, u32[]{:S(2)}, u32[]{:S(2)}) async-start(f32[32,9,128]{2,1,0:T(8,128)} %copy.134), calls=%async_computation.2 | async-start | bytes 524288 | tf_op jit(solution)/shard_map/all_to_all | solution.py:131
Sparse Core Ops, SparseCore 0:
  10.9 84.6 all-gather.1

commit v2 on v1

--- a/solution.py
+++ b/solution.py
@@ -66,16 +66,12 @@
 
     query_heads = query.reshape(H, HD).astype(f32)
     wq_rows = jnp.sum(key_weight.reshape(rows, H, HD).astype(f32) * query_heads[None], axis=2)
-    wq_hi, wq_lo = split(wq_rows)
-    pad = (-(2 * width + 2 * H)) % 128
-    packed = jnp.concatenate(
-        [value_weight, out_weight, wq_hi, wq_lo, jnp.zeros((rows, pad), bf16)], axis=1
-    )
-    full = lax.all_gather(packed, "tok", axis=0, tiled=True)
-    value_matrix = full[:, :width]
-    out_matrix = full[:, width : 2 * width]
-    wq_hi = full[:, 2 * width : 2 * width + H]
-    wq_lo = full[:, 2 * width + H : 2 * width + 2 * H]
+    wq_copies = jnp.broadcast_to(wq_rows[None], (n_tok, rows, H))
+    wq_full = lax.all_to_all(wq_copies, "tok", 0, 0, tiled=True).reshape(n_tok * rows, H)
+    wq_hi, wq_lo = split(wq_full)
+    full = lax.all_gather(jnp.stack([value_weight, out_weight]), "tok", axis=1, tiled=True)
+    value_matrix = full[0]
+    out_matrix = full[1]
 
     slot_pixels = lax.all_to_all(patches, "var", 2, 0, tiled=True)
     live_slot = live_index(slot_var, var_total)

time: 187 us -> 190 us (1.016)
  waiting for transfers between devices: 93.8 us -> 75.3 us
  starting transfers between devices: 14.7 us -> 25.8 us
  matrix products: 37 us -> 41.6 us
  other arithmetic: 7.18 us -> 10.8 us
  local copies, waits for them, and re-layouts: 19.2 us -> 21.7 us
    all_gather x1, waiting for transfers between devices: 68.8 us -> 48.1 us  [body(): lax.all_gather(jnp.stack([value_weight, out_weight]), 'tok', axis=1, tile...]
    all_to_all x0 -> x1, starting transfers between devices: none -> 11.2 us  [body(): lax.all_to_all(wq_copies, 'tok', 0, 0, tiled=True).reshape(n_tok * rows, H)]
    all_to_all x0 -> x1, waiting for transfers between devices: none -> 5.08 us  [body(): lax.all_to_all(wq_copies, 'tok', 0, 0, tiled=True).reshape(n_tok * rows, H)]
    dot_general x14, matrix products: 29.2 us -> 33.6 us  [ein(): return jnp.einsum(spec, a, b, preferred_element_type=f32)]
    all_to_all x1, waiting for transfers between devices: 2.77 us -> 0.01 us  [body(): slot_pixels = lax.all_to_all(patches, 'var', 2, 0, tiled=True)]
    unnamed x17 -> x50, local copies, waits for them, and re-layouts: 4.92 us -> 5.65 us
  transfers between devices with their start and end apart: 4 -> 5, of which waited for: 4 -> 4; matrix products, arithmetic and copies ran while one was open for 9% -> 12% of each run, Pallas kernels for 0% -> 0%
where the time goes in v2:
time: 190 us
  waiting for transfers between devices  75.3 us (40%)
  matrix products  41.6 us (22%)
  starting transfers between devices  25.8 us (14%)
  local copies, waits for them, and re-layouts  21.7 us (11%)
  between operations  14.4 us (8%)
  other arithmetic  10.8 us (6%)
    all_gather x1, waiting for transfers between devices, body(): lax.all_gather(jnp.stack([value_weight, out_weight]), 'tok', axis=1, tile...  48.1 us
    dot_general x14, matrix products, ein(): return jnp.einsum(spec, a, b, preferred_element_type=f32)  33.6 us
    all_to_all x1, waiting for transfers between devices, body(): by_var = lax.all_to_all(blocks, 'var', 0, 0, tiled=True).sum(axis=0)  13.6 us
    all_to_all x1, starting transfers between devices, body(): lax.all_to_all(wq_copies, 'tok', 0, 0, tiled=True).reshape(n_tok * rows, H)  11.2 us
    all_to_all x1, waiting for transfers between devices, body(): by_tok = lax.all_to_all(by_var, 'tok', 0, 0, tiled=True).sum(axis=0)  8.57 us
    slice x2, local copies, waits for them, and re-layouts, body(): value_matrix = full[0]  6.18 us
    all_to_all x1, starting transfers between devices, body(): by_tok = lax.all_to_all(by_var, 'tok', 0, 0, tiled=True).sum(axis=0)  5.8 us
    unnamed x50, local copies, waits for them, and re-layouts  5.65 us
  transfers between devices with their start and end apart: 5, of which 4 were waited for; matrix products, arithmetic and copies ran while one was open for 12% of the time, Pallas kernels for 0%

profile of v2, /device:TPU:32, one launch (start us, length us, event | category | flops | bytes accessed | tf_op | source)
XLA Modules:
  0.0 189.6 jit_solution(7815867198240021874)
XLA Ops:
  7.2 1.6 pad_maximum_fusion
  8.8 0.9 copy.110
  9.7 0.8 reshape.93
  10.5 4.5 %all-to-all-start.1 = ((bf16[8,2,288]{2,1,0:T(2,128)(2,1)}), bf16[8,2,288]{2,1,0:T(2,128)(2,1)S(1)}, u32[]{:S(2)}, u32[]{:S(2)}) async-start(bf16[8,2,288]{2,1,0:T(2,128)(2,1)} %reshape.93), calls=%async_computation.1 | async-start | bytes 24576 | tf_op jit(solution)/shard_map/all_to_all | solution.py:76
  15.0 1.0 reshape.72
  15.9 0.8 reshape.73
  16.9 0.8 select_reduce_fusion
  17.7 0.7 compare_and_fusion
  18.4 0.9 convert_element_type.88
  19.4 0.8 reshape.95
  20.2 0.7 broadcast_in_dim.69
  20.9 11.2 %all-to-all-start = ((f32[32,1,512]{2,1,0:T(1,128)}), f32[32,1,512]{2,1,0:T(1,128)S(1)}, u32[]{:S(2)}, u32[]{:S(2)}) async-start(f32[32,1,512]{2,1,0:T(1,128)} %reshape.95), calls=%async_computation | async-start | bytes 131072 | tf_op jit(solution)/shard_map/all_to_all | solution.py:70
  33.4 2.9 %multiply_convert_fusion = (bf16[48,16,1024]{2,1,0:T(8,128)(2,1)S(1)}, f32[48,16,1024]{2,1,0:T(8,128)}) fusion(f32[48,1024]{1,0:T(8,128)S(1)} %convert_element_type.88, bf16[48,4,1024]{2,1,0:T(4,128)(2,1)S(1)} %copy-done, bf16[48,4,16]{2,1,0:T(4,128)(2,1)S(1)} %gather_fusion, pred[48]{0:T(512)(128)(4,1)S(1)} %compare_and_fusion.1), kind=kOutput, calls=%fused_computation.17 | convolution fusion | flops 11013120 | bytes 5314608 | tf_op jit(solution)/shard_map/vpt,vpd->vtd/dot_general | solution.py:45
  36.4 5.1 %all-to-all-done = f32[32,1,512]{2,1,0:T(1,128)S(1)} async-done(((f32[32,1,512]{2,1,0:T(1,128)}), f32[32,1,512]{2,1,0:T(1,128)S(1)}, u32[]{:S(2)}, u32[]{:S(2)}) %all-to-all-start) | async-done | bytes 65568 | tf_op jit(solution)/shard_map/all_to_all | solution.py:70
  42.0 0.8 reduce
  43.1 1.0 fusion.35
  44.1 1.1 bitcast_reduce_fusion
  45.2 0.7 copy-done.14
  45.9 0.7 fusion.59
  46.6 48.1 %all-gather.2.cloned.1.call-done = bf16[2,1024,1024]{2,1,0:T(8,128)(2,1)} async-done(((bf16[2,32,1024]{2,1,0:T(8,128)(2,1)}), bf16[2,1024,1024]{2,1,0:T(8,128)(2,1)}) %all-gather.2.cloned.1.call-update) | async-done | bytes 4194320 | tf_op jit(solution)/shard_map/all_gather | solution.py:72
  94.7 3.1 %slice.12 = bf16[1,1024,1024]{2,1,0:T(8,128)(2,1)} slice(bf16[2,1024,1024]{2,1,0:T(8,128)(2,1)} %all-gather.2.cloned.1.call-done), slice={[0:1], [0:1024], [0:1024]} | slice | bytes 4194304 | tf_op jit(solution)/shard_map/slice | solution.py:73
  97.8 3.0 %copy.107 = bf16[1,1024,1024]{1,2,0:T(8,128)(2,1)S(1)} copy(bf16[1,1024,1024]{2,1,0:T(8,128)(2,1)} %slice.12) | data formatting | bytes 4194304 | tf_op jit(solution)/shard_map/slice | solution.py:73
  100.9 2.2 %fusion.28 = bf16[16,1024]{1,0:T(8,128)(2,1)S(1)} fusion(bf16[16,1024]{1,0:T(8,128)(2,1)S(1)} %copy-done.20, bf16[2,1024,1024]{2,1,0:T(8,128)(2,1)} %all-gather.2.cloned.1.call-done), kind=kOutput, calls=%fused_computation.42 | convolution fusion | flops 33570816 | bytes 2162688 | tf_op jit(solution)/shard_map/dot_general | solution.py:99
  103.1 0.8 reshape.70
  103.9 1.4 subtract_convert_fusion
  105.3 1.5 fusion.30
  106.8 2.6 %convolution_add_fusion.2 = f32[16,48,16]{1,2,0:T(8,128)S(1)} fusion(f32[16,48,16]{1,2,0:T(8,128)S(1)} %fusion.30, bf16[48,16,1024]{2,1,0:T(8,128)(2,1)S(1)} %copy-done.2, bf16[16,16,1024]{2,0,1:T(8,128)(2,1)S(1)} %get-tuple-element.8), kind=kOutput, calls=%fused_computation.37 | convolution fusion | flops 25178112 | bytes 2195456 | tf_op jit(solution)/shard_map/vtd,thd->tvh/dot_general | solution.py:45
  109.4 1.9 %subtract_convert_fusion.2 = (bf16[16,48,16]{1,2,0:T(8,128)(2,1)}, bf16[16,48,16]{1,2,0:T(8,128)(2,1)}) fusion(f32[16,48,16]{1,0,2:T(8,128)S(1)} %copy-done.15, f32[16,48,16]{1,2,0:T(8,128)S(1)} %convolution_add_fusion.2, f32[16,16]{1,0:T(8,128)S(1)} %get-tuple-element.13), kind=kOutput, calls=%fused_computation.67 | output fusion | flops 184623 | bytes 148480 | tf_op jit(solution)/shard_map/sub | solution.py:106
  111.3 1.7 copy.128
  113.0 3.3 %fusion.56 = f32[1024,16,48]{0,1,2:T(8,128)} fusion(bf16[16,48,16]{2,0,1:T(8,128)(2,1)} %copy.128, f32[1024,16]{0,1:T(8,128)} %copy-done.5), kind=kOutput, calls=%fused_computation.84 | convolution fusion | flops 25231360 | bytes 3235840 | tf_op jit(solution)/shard_map/tvh,dh->vtd/dot_general | solution.py:45
  116.4 2.3 %fusion.50 = f32[1024,16,48]{0,1,2:T(8,128)} fusion(bf16[16,48,16]{2,0,1:T(8,128)(2,1)S(1)} %copy-done.4, f32[1024,16]{0,1:T(8,128)S(1)} %copy-done.6), kind=kOutput, calls=%fused_computation.76 | convolution fusion | flops 25182208 | bytes 3235840 | tf_op jit(solution)/shard_map/tvh,dh->vtd/dot_general | solution.py:45
  118.7 2.2 %fusion.41 = f32[16,1024,48]{1,2,0:T(8,128)} fusion(bf16[16,48,16]{1,2,0:T(8,128)(2,1)S(1)} %copy-done.8, bf16[16,16,1024]{2,0,1:T(8,128)(2,1)S(1)} %get-tuple-element.8), kind=kOutput, calls=%fused_computation.57 | convolution fusion | flops 25165824 | bytes 3694592 | tf_op jit(solution)/shard_map/tvh,thd->vtd/dot_general | solution.py:45
  120.9 2.3 %fusion.44 = f32[16,1024,48]{1,2,0:T(8,128)} fusion(bf16[16,48,16]{1,2,0:T(8,128)(2,1)S(1)} %copy-done.8, bf16[16,16,1024]{2,0,1:T(8,128)(2,1)S(1)} %get-tuple-element.9), kind=kOutput, calls=%fused_computation.60 | convolution fusion | flops 25165824 | bytes 3694592 | tf_op jit(solution)/shard_map/tvh,thd->vtd/dot_general | solution.py:45
  123.4 8.5 %fusion.8 = bf16[48,16,1024]{2,1,0:T(8,128)(2,1)S(1)} fusion(f32[1024,16,48]{0,1,2:T(8,128)} %fusion.56, f32[1024,16,48]{0,1,2:T(8,128)} %fusion.50, f32[16,1024,48]{1,2,0:T(8,128)} %fusion.41, f32[16,1024,48]{1,2,0:T(8,128)} %fusion.44, bf16[16,48,16]{2,0,1:T(8,128)(2,1)S(1)} %copy.130, f32[1024,16]{0,1:T(8,128)S(1)} %copy-done.7), kind=kOutput, calls=%fused_computation.11 | convolution fusion | flops 29114368 | bytes 14245888 | tf_op jit(solution)/shard_map/tvh,dh->vtd/dot_general | solution.py:45
  131.9 3.2 %fusion.6 = f32[48,4,1024]{2,1,0:T(4,128)S(1)} fusion(bf16[48,16,1024]{2,1,0:T(8,128)(2,1)S(1)} %fusion.8, f32[48,16,1024]{2,1,0:T(8,128)S(1)} %copy-done.3, f32[48,1024]{1,0:T(8,128)S(1)} %copy-done.11, bf16[48,4,16]{2,1,0:T(4,128)(2,1)S(1)} %copy-done.13, pred[48]{0:T(512)(128)(4,1)S(1)} %copy-done.19), kind=kOutput, calls=%fused_computation.9 | convolution fusion | flops 46402560 | bytes 5707824 | tf_op jit(solution)/shard_map/vpt,vtd->vpd/dot_general | solution.py:117
  135.6 2.0 %gather_fusion.1 = f32[72,4096]{1,0:T(8,128)} fusion(f32[48,4096]{1,0:T(8,128)S(1)} %bitcast.98, s32[1024]{0:T(1024)S(1)} %pad_clamp_fusion), kind=kCustom, calls=%fused_computation.1 | custom fusion | bytes 2359584 | tf_op jit(solution)/shard_map/jit(_take)/gather | solution.py:124
  137.6 1.5 copy.134
  139.1 1.3 select_bitcast_fusion
  140.4 4.3 %all-to-all-start.2 = ((f32[8,32,9,128]{3,1,2,0:T(8,128)}), f32[8,32,9,128]{3,1,2,0:T(8,128)}, u32[]{:S(2)}, u32[]{:S(2)}) async-start(f32[8,32,9,128]{3,1,2,0:T(8,128)} %select_bitcast_fusion), calls=%async_computation.2 | async-start | bytes 2359296 | tf_op jit(solution)/shard_map/all_to_all | solution.py:126
  144.7 3.2 %subtract_convert_fusion.1 = (bf16[16,16,1024]{2,1,0:T(8,128)(2,1)S(1)}, bf16[16,16,1024]{2,1,0:T(8,128)(2,1)S(1)}) fusion(bf16[16,48,16]{1,2,0:T(8,128)(2,1)S(1)} %copy-done.9, bf16[48,16,1024]{2,1,0:T(8,128)(2,1)} %copy-done.1), kind=kOutput, calls=%fused_computation.44 | convolution fusion | flops 26214400 | bytes 2646016 | tf_op jit(solution)/shard_map/tvh,vtd->thd/dot_general | solution.py:45
  147.9 0.6 fusion.38
  148.5 13.6 %all-to-all-done.2 = f32[8,32,9,128]{3,1,2,0:T(8,128)} async-done(((f32[8,32,9,128]{3,1,2,0:T(8,128)}), f32[8,32,9,128]{3,1,2,0:T(8,128)}, u32[]{:S(2)}, u32[]{:S(2)}) %all-to-all-start.2) | async-done | bytes 1179680 | tf_op jit(solution)/shard_map/all_to_all | solution.py:126
  162.1 1.4 reduce_sum.61
  163.5 0.8 copy.131
  164.3 5.8 %all-to-all-start.3 = ((f32[32,9,128]{2,1,0:T(8,128)}), f32[32,9,128]{2,1,0:T(8,128)S(1)}, u32[]{:S(2)}, u32[]{:S(2)}) async-start(f32[32,9,128]{2,1,0:T(8,128)} %copy.131), calls=%async_computation.3 | async-start | bytes 524288 | tf_op jit(solution)/shard_map/all_to_all | solution.py:127
  170.1 0.7 fusion.25
  170.9 2.6 %fusion.26 = bf16[16,1024]{1,0:T(8,128)(2,1)} fusion(bf16[16,1024]{1,0:T(8,128)(2,1)S(1)} %reshape.69, bf16[2,1024,1024]{2,1,0:T(8,128)(2,1)} %all-gather.2.cloned.1.call-done), kind=kOutput, calls=%fused_computation.40 | convolution fusion | flops 33570816 | bytes 2162688 | tf_op jit(solution)/shard_map/dot_general | solution.py:96
  173.5 8.6 %all-to-all-done.3 = f32[32,9,128]{2,1,0:T(8,128)S(1)} async-done(((f32[32,9,128]{2,1,0:T(8,128)}), f32[32,9,128]{2,1,0:T(8,128)S(1)}, u32[]{:S(2)}, u32[]{:S(2)}) %all-to-all-start.3) | async-done | bytes 147488 | tf_op jit(solution)/shard_map/all_to_all | solution.py:127
  (65 shorter events, 4.2 us)
Async XLA Ops:
  7.2 26.2 %copy-start = (bf16[48,4,1024]{2,1,0:T(4,128)(2,1)S(1)}, bf16[48,4,1024]{2,1,0:T(4,128)(2,1)}, u32[]{:S(2)}) copy-start(bf16[48,4,1024]{2,1,0:T(4,128)(2,1)} %param.11) | copy-start | bytes 1179652
  7.2 87.5 %all-gather.2.cloned.1.call-start = ((), (), s32[]{:S(2)}) async-start(), calls=%async_computation.4 | async-start | bytes 4325376 | tf_op jit(solution)/shard_map/all_gather | solution.py:72
  10.5 10.4 %all-to-all-start.1 = ((bf16[8,2,288]{2,1,0:T(2,128)(2,1)}), bf16[8,2,288]{2,1,0:T(2,128)(2,1)S(1)}, u32[]{:S(2)}, u32[]{:S(2)}) async-start(bf16[8,2,288]{2,1,0:T(2,128)(2,1)} %reshape.93), calls=%async_computation.1 | async-start | bytes 24576 | tf_op jit(solution)/shard_map/all_to_all | solution.py:76
  17.7 18.6 %copy-start.18 = (pred[48]{0:T(512)(128)(4,1)}, pred[48]{0:T(512)(128)(4,1)S(1)}, u32[]{:S(2)}) copy-start(pred[48]{0:T(512)(128)(4,1)S(1)} %compare_and_fusion.1) | copy-start | bytes 148
  19.3 17.0 %copy-start.10 = (f32[48,1024]{1,0:T(8,128)}, f32[48,1024]{1,0:T(8,128)S(1)}, u32[]{:S(2)}) copy-start(f32[48,1024]{1,0:T(8,128)S(1)} %convert_element_type.88) | copy-start | bytes 589828
  20.9 20.6 %all-to-all-start = ((f32[32,1,512]{2,1,0:T(1,128)}), f32[32,1,512]{2,1,0:T(1,128)S(1)}, u32[]{:S(2)}, u32[]{:S(2)}) async-start(f32[32,1,512]{2,1,0:T(1,128)} %reshape.95), calls=%async_computation | async-start | bytes 131072 | tf_op jit(solution)/shard_map/all_to_all | solution.py:70
  33.4 8.0 %copy-start.12 = (bf16[48,4,16]{2,1,0:T(4,128)(2,1)}, bf16[48,4,16]{2,1,0:T(4,128)(2,1)S(1)}, u32[]{:S(2)}) copy-start(bf16[48,4,16]{2,1,0:T(4,128)(2,1)S(1)} %gather_fusion) | copy-start | bytes 18436
  36.4 58.3 %copy-start.1 = (bf16[48,16,1024]{2,1,0:T(8,128)(2,1)}, bf16[48,16,1024]{2,1,0:T(8,128)(2,1)S(1)}, u32[]{:S(2)}) copy-start(bf16[48,16,1024]{2,1,0:T(8,128)(2,1)S(1)} %get-tuple-element.11) | copy-start | bytes 4718596
  43.1 51.6 %copy-start.5 = (f32[1024,16]{0,1:T(8,128)}, f32[1024,16]{0,1:T(8,128)S(1)}, u32[]{:S(2)}) copy-start(f32[1024,16]{0,1:T(8,128)S(1)} %reshape.68) | copy-start | bytes 196612
  45.2 0.7 copy-start.14
  46.6 54.3 %copy-start.20 = (bf16[16,1024]{1,0:T(8,128)(2,1)S(1)}, bf16[16,1024]{1,0:T(8,128)(2,1)}, u32[]{:S(2)}) copy-start(bf16[16,1024]{1,0:T(8,128)(2,1)} %param.17) | copy-start | bytes 98308
  103.9 1.4 copy-start.2
  105.2 4.2 %copy-start.15 = (f32[16,48,16]{1,0,2:T(8,128)S(1)}, f32[16,48,16]{1,0,2:T(8,128)}, u32[]{:S(2)}) copy-start(f32[16,48,16]{1,0,2:T(8,128)} %copy-done.14) | copy-start | bytes 147460
  113.0 3.3 %copy-start.4 = (bf16[16,48,16]{2,0,1:T(8,128)(2,1)S(1)}, bf16[16,48,16]{2,0,1:T(8,128)(2,1)}, u32[]{:S(2)}) copy-start(bf16[16,48,16]{2,0,1:T(8,128)(2,1)} %copy.128) | copy-start | bytes 73732
  113.0 3.3 %copy-start.6 = (f32[1024,16]{0,1:T(8,128)S(1)}, f32[1024,16]{0,1:T(8,128)}, u32[]{:S(2)}) copy-start(f32[1024,16]{0,1:T(8,128)} %copy-done.5) | copy-start | bytes 196612
  113.0 5.6 %copy-start.8 = (bf16[16,48,16]{1,2,0:T(8,128)(2,1)S(1)}, bf16[16,48,16]{1,2,0:T(8,128)(2,1)}, u32[]{:S(2)}) copy-start(bf16[16,48,16]{1,2,0:T(8,128)(2,1)} %fusion.59) | copy-start | bytes 73732
  120.9 2.3 %copy-start.16 = (bf16[16,48,16]{1,2,0:T(8,128)(2,1)S(1)}, bf16[16,48,16]{1,2,0:T(8,128)(2,1)}, u32[]{:S(2)}) copy-start(bf16[16,48,16]{1,2,0:T(8,128)(2,1)} %get-tuple-element.4) | copy-start | bytes 73732
  120.9 2.5 %copy-start.7 = (f32[1024,16]{0,1:T(8,128)S(1)}, f32[1024,16]{0,1:T(8,128)}, u32[]{:S(2)}) copy-start(f32[1024,16]{0,1:T(8,128)} %copy-done.5) | copy-start | bytes 196612
  123.4 8.5 %copy-start.3 = (f32[48,16,1024]{2,1,0:T(8,128)S(1)}, f32[48,16,1024]{2,1,0:T(8,128)}, u32[]{:S(2)}) copy-start(f32[48,16,1024]{2,1,0:T(8,128)} %get-tuple-element.12) | copy-start | bytes 9437188
  123.4 8.5 %copy-start.11 = (f32[48,1024]{1,0:T(8,128)S(1)}, f32[48,1024]{1,0:T(8,128)}, u32[]{:S(2)}) copy-start(f32[48,1024]{1,0:T(8,128)} %copy-done.10) | copy-start | bytes 589828
  123.4 8.5 %copy-start.13 = (bf16[48,4,16]{2,1,0:T(4,128)(2,1)S(1)}, bf16[48,4,16]{2,1,0:T(4,128)(2,1)}, u32[]{:S(2)}) copy-start(bf16[48,4,16]{2,1,0:T(4,128)(2,1)} %copy-done.12) | copy-start | bytes 18436
  123.4 8.5 %copy-start.19 = (pred[48]{0:T(512)(128)(4,1)S(1)}, pred[48]{0:T(512)(128)(4,1)}, u32[]{:S(2)}) copy-start(pred[48]{0:T(512)(128)(4,1)} %copy-done.18) | copy-start | bytes 148
  135.6 3.5 %copy-start.17 = (pred[8,9]{1,0:T(8,128)(4,1)S(1)}, pred[8,9]{1,0:T(8,128)(4,1)}, u32[]{:S(2)}) copy-start(pred[8,9]{1,0:T(8,128)(4,1)} %broadcast_in_dim.69) | copy-start | bytes 220
  137.6 7.1 %copy-start.9 = (bf16[16,48,16]{1,2,0:T(8,128)(2,1)S(1)}, bf16[16,48,16]{1,2,0:T(8,128)(2,1)}, u32[]{:S(2)}) copy-start(bf16[16,48,16]{1,2,0:T(8,128)(2,1)} %fusion.59) | copy-start | bytes 73732
  140.4 21.7 %all-to-all-start.2 = ((f32[8,32,9,128]{3,1,2,0:T(8,128)}), f32[8,32,9,128]{3,1,2,0:T(8,128)}, u32[]{:S(2)}, u32[]{:S(2)}) async-start(f32[8,32,9,128]{3,1,2,0:T(8,128)} %select_bitcast_fusion), calls=%async_computation.2 | async-start | bytes 2359296 | tf_op jit(solution)/shard_map/all_to_all | solution.py:126
  164.3 17.8 %all-to-all-start.3 = ((f32[32,9,128]{2,1,0:T(8,128)}), f32[32,9,128]{2,1,0:T(8,128)S(1)}, u32[]{:S(2)}, u32[]{:S(2)}) async-start(f32[32,9,128]{2,1,0:T(8,128)} %copy.131), calls=%async_computation.3 | async-start | bytes 524288 | tf_op jit(solution)/shard_map/all_to_all | solution.py:127
Sparse Core Ops, SparseCore 0:
  10.6 84.0 all-gather.1

commit v3 on v2

--- a/solution.py
+++ b/solution.py
@@ -96,23 +96,23 @@
     mixed_out = jnp.dot(pooled, out_matrix, preferred_element_type=f32).astype(bf16)
     contract = (((1,), (1,)), ((), ()))
     grad_pooled = (
-        lax.dot_general(cotangent, out_matrix, contract, preferred_element_type=f32)
-        .astype(bf16)
+        lax.dot_general(out_matrix, cotangent, contract, preferred_element_type=f32)
+        .T.astype(bf16)
         .reshape(tok_count, H, HD)
     )
     spread = ein("thj,dhj->thd", grad_pooled, value_heads)
     spread_hi, spread_lo = split(spread)
-    grad_attn = ein("vtd,thd->tvh", embedded, spread_hi) + ein("vtd,thd->tvh", embedded, spread_lo)
+    both = ein("vtd,thd->tvh", embedded, jnp.concatenate([spread_hi, spread_lo], axis=1))
+    grad_attn = both[:, :, :H] + both[:, :, H:]
     grad_scores = attn_f32 * (grad_attn - jnp.sum(attn_f32 * grad_attn, axis=1, keepdims=True))
     grad_raw = grad_scores * (1.0 - squashed * squashed) / math.sqrt(HD)
     raw_hi, raw_lo = split(grad_raw)
-    grad_embed = (
-        ein("tvh,thd->vtd", attn_bf, spread_hi)
-        + ein("tvh,thd->vtd", attn_bf, spread_lo)
-        + ein("tvh,dh->vtd", raw_hi, wq_hi)
-        + ein("tvh,dh->vtd", raw_hi, wq_lo)
-        + ein("tvh,dh->vtd", raw_lo, wq_hi)
-    ).astype(bf16)
+    left = jnp.concatenate([attn_bf, attn_bf, raw_hi, raw_hi, raw_lo], axis=2)
+    wq_t = jnp.concatenate([wq_hi.T, wq_lo.T, wq_hi.T], axis=0)
+    right = jnp.concatenate(
+        [spread_hi, spread_lo, jnp.broadcast_to(wq_t[None], (tok_count,) + wq_t.shape)], axis=1
+    )
+    grad_embed = ein("tvk,tkd->vtd", left, right).astype(bf16)
     grad_pre = grad_embed.astype(f32) * gelu_slope(pre_act)
     partial = jnp.einsum(
         "vpt,vtd->vpd", pixels.astype(f32), grad_pre, precision=lax.Precision.HIGHEST

time: 190 us -> 170 us (0.89)
  matrix products: 41.6 us -> 20.6 us
    dot_general x14 -> x9, matrix products: 33.6 us -> 12 us  [ein(): return jnp.einsum(spec, a, b, preferred_element_type=f32)]
    unnamed x50 -> x23, local copies, waits for them, and re-layouts: 5.65 us -> 6.81 us
  transfers between devices with their start and end apart: 5 -> 5, of which waited for: 4 -> 4; matrix products, arithmetic and copies ran while one was open for 12% -> 13% of each run, Pallas kernels for 0% -> 0%
where the time goes in v3:
time: 170 us; the launch traced here: 169 us
  waiting for transfers between devices  77 us (45%)
  starting transfers between devices  25.9 us (15%)
  matrix products  20.6 us (12%)
  local copies, waits for them, and re-layouts  20.3 us (12%)
  between operations  14.3 us (8%)
  other arithmetic  11.1 us (7%)
    all_gather x1, waiting for transfers between devices, body(): lax.all_gather(jnp.stack([value_weight, out_weight]), 'tok', axis=1, tile...  49.7 us
    all_to_all x1, waiting for transfers between devices, body(): by_var = lax.all_to_all(blocks, 'var', 0, 0, tiled=True).sum(axis=0)  13.5 us
    dot_general x9, matrix products, ein(): return jnp.einsum(spec, a, b, preferred_element_type=f32)  12 us
    all_to_all x1, starting transfers between devices, body(): lax.all_to_all(wq_copies, 'tok', 0, 0, tiled=True).reshape(n_tok * rows, H)  11.2 us
    all_to_all x1, waiting for transfers between devices, body(): by_tok = lax.all_to_all(by_var, 'tok', 0, 0, tiled=True).sum(axis=0)  8.57 us
    unnamed x23, local copies, waits for them, and re-layouts  6.81 us
    slice x2, local copies, waits for them, and re-layouts, body(): value_matrix = full[0]  6.01 us
    all_to_all x1, starting transfers between devices, body(): by_tok = lax.all_to_all(by_var, 'tok', 0, 0, tiled=True).sum(axis=0)  5.81 us
  transfers between devices with their start and end apart: 5, of which 4 were waited for; matrix products, arithmetic and copies ran while one was open for 13% of the time, Pallas kernels for 0%

profile of v3, /device:TPU:32, one launch (start us, length us, event | category | flops | bytes accessed | tf_op | source)
XLA Modules:
  0.0 169.3 jit_solution(8375343561235493912)
XLA Ops:
  7.2 1.6 pad_maximum_fusion.1
  8.8 0.9 copy.95
  9.7 0.8 reshape.94
  10.5 4.5 %all-to-all-start.1 = ((bf16[8,2,288]{2,1,0:T(2,128)(2,1)}), bf16[8,2,288]{2,1,0:T(2,128)(2,1)S(1)}, u32[]{:S(2)}, u32[]{:S(2)}) async-start(bf16[8,2,288]{2,1,0:T(2,128)(2,1)} %reshape.94), calls=%async_computation.1 | async-start | bytes 24576 | tf_op jit(solution)/shard_map/all_to_all | solution.py:76
  15.0 1.0 reshape.73
  15.9 0.8 reshape.74
  16.9 0.8 select_reduce_fusion
  17.7 0.7 compare_and_fusion
  18.4 0.9 convert_element_type.92
  19.3 0.8 reshape.96
  20.3 11.2 %all-to-all-start = ((f32[32,1,512]{2,1,0:T(1,128)}), f32[32,1,512]{2,1,0:T(1,128)S(1)}, u32[]{:S(2)}, u32[]{:S(2)}) async-start(f32[32,1,512]{2,1,0:T(1,128)} %reshape.96), calls=%async_computation | async-start | bytes 131072 | tf_op jit(solution)/shard_map/all_to_all | solution.py:70
  31.5 0.3 reshape.95
  31.9 0.3 copy.113
  32.2 0.6 gather_fusion
  32.8 2.9 %multiply_convert_fusion = (bf16[48,16,1024]{2,1,0:T(8,128)(2,1)S(1)}, f32[48,16,1024]{2,1,0:T(8,128)}) fusion(f32[48,1024]{1,0:T(8,128)S(1)} %convert_element_type.92, bf16[48,4,1024]{2,1,0:T(4,128)(2,1)S(1)} %copy-done, bf16[48,4,16]{2,1,0:T(4,128)(2,1)S(1)} %gather_fusion, pred[48]{0:T(512)(128)(4,1)S(1)} %compare_and_fusion.1), kind=kOutput, calls=%fused_computation.14 | convolution fusion | flops 11013120 | bytes 5314608 | tf_op jit(solution)/shard_map/vpt,vpd->vtd/dot_general | solution.py:45
  35.8 5.2 %all-to-all-done = f32[32,1,512]{2,1,0:T(1,128)S(1)} async-done(((f32[32,1,512]{2,1,0:T(1,128)}), f32[32,1,512]{2,1,0:T(1,128)S(1)}, u32[]{:S(2)}, u32[]{:S(2)}) %all-to-all-start) | async-done | bytes 65568 | tf_op jit(solution)/shard_map/all_to_all | solution.py:70
  41.0 0.5 broadcast.114
  41.5 0.8 reduce
  42.7 1.0 fusion.41
  43.6 1.1 bitcast_reduce_fusion
  44.9 49.7 %all-gather.2.cloned.1.call-done = bf16[2,1024,1024]{2,1,0:T(8,128)(2,1)} async-done(((bf16[2,32,1024]{2,1,0:T(8,128)(2,1)}), bf16[2,1024,1024]{2,1,0:T(8,128)(2,1)}) %all-gather.2.cloned.1.call-update) | async-done | bytes 4194320 | tf_op jit(solution)/shard_map/all_gather | solution.py:72
  94.7 3.1 %slice.20 = bf16[1,1024,1024]{2,1,0:T(8,128)(2,1)} slice(bf16[2,1024,1024]{2,1,0:T(8,128)(2,1)} %all-gather.2.cloned.1.call-done), slice={[0:1], [0:1024], [0:1024]} | slice | bytes 4194304 | tf_op jit(solution)/shard_map/slice | solution.py:73
  97.8 2.9 %copy.92 = bf16[1,1024,1024]{1,2,0:T(8,128)(2,1)S(1)} copy(bf16[1,1024,1024]{2,1,0:T(8,128)(2,1)} %slice.20) | data formatting | bytes 4194304 | tf_op jit(solution)/shard_map/slice | solution.py:73
  100.7 2.2 %fusion.34 = bf16[16,1024]{1,0:T(8,128)(2,1)S(1)} fusion(bf16[16,1024]{1,0:T(8,128)(2,1)S(1)} %copy-done.6, bf16[2,1024,1024]{2,1,0:T(8,128)(2,1)} %all-gather.2.cloned.1.call-done), kind=kOutput, calls=%fused_computation.44 | convolution fusion | flops 33570816 | bytes 2162688 | tf_op jit(solution)/shard_map/dot_general | solution.py:99
  103.1 0.4 subtract_convert_fusion
  103.5 0.3 copy.106
  103.9 0.3 copy.105
  104.2 0.7 copy-done.2
  104.9 1.5 fusion.35
  106.4 2.7 %constant_dynamic-update-slice_fusion.1 = (bf16[16,48,80]{1,2,0:T(8,128)(2,1)S(1)}, f32[16,48,16]{1,2,0:T(8,128)S(1)}) fusion(bf16[16,48,80]{1,2,0:T(8,128)(2,1)S(1)} %copy-done.5, f32[16,48,16]{1,0,2:T(8,128)S(1)} %get-tuple-element.16, f32[16,48,32]{1,2,0:T(8,128)S(1)} %fusion.35, f32[16,16]{1,0:T(8,128)S(1)} %get-tuple-element.15), kind=kOutput, calls=%fused_computation.79 | output fusion | flops 172335 | bytes 999424 | tf_op jit(solution)/shard_map/sub | solution.py:107
  109.3 0.6 fusion.12
  109.9 1.3 copy-done.3
  111.2 3.8 %fusion.6 = f32[48,4,1024]{2,1,0:T(4,128)S(1)} fusion(f32[48,16,1024]{2,1,0:T(8,128)S(1)} %copy-done.3, bf16[16,1024,48]{1,2,0:T(8,128)(2,1)S(1)} %fusion.12, f32[48,1024]{1,0:T(8,128)S(1)} %convert_element_type.92, bf16[48,4,16]{2,1,0:T(4,128)(2,1)S(1)} %gather_fusion, pred[48]{0:T(512)(128)(4,1)S(1)} %compare_and_fusion.1), kind=kOutput, calls=%fused_computation.9 | convolution fusion | flops 46402560 | bytes 5707824 | tf_op jit(solution)/shard_map/vpt,vtd->vpd/dot_general | solution.py:117
  114.9 0.5 copy.114
  115.4 1.9 %gather_fusion.1 = f32[72,4096]{1,0:T(8,128)} fusion(f32[48,4096]{1,0:T(8,128)S(1)} %bitcast.85, s32[1024]{0:T(1024)S(1)} %get-tuple-element.19), kind=kCustom, calls=%fused_computation.1 | custom fusion | bytes 2359584 | tf_op jit(solution)/shard_map/jit(_take)/gather | solution.py:124
  117.3 1.5 copy.115
  118.8 1.3 select_bitcast_fusion
  120.1 4.4 %all-to-all-start.2 = ((f32[8,32,9,128]{3,1,2,0:T(8,128)}), f32[8,32,9,128]{3,1,2,0:T(8,128)}, u32[]{:S(2)}, u32[]{:S(2)}) async-start(f32[8,32,9,128]{3,1,2,0:T(8,128)} %select_bitcast_fusion), calls=%async_computation.2 | async-start | bytes 2359296 | tf_op jit(solution)/shard_map/all_to_all | solution.py:126
  124.5 3.2 %subtract_convert_fusion.1 = (bf16[16,16,1024]{2,1,0:T(8,128)(2,1)S(1)}, bf16[16,16,1024]{2,1,0:T(8,128)(2,1)S(1)}) fusion(bf16[16,48,16]{1,2,0:T(8,128)(2,1)S(1)} %get-tuple-element.7, bf16[48,16,1024]{2,1,0:T(8,128)(2,1)} %copy-done.1), kind=kOutput, calls=%fused_computation.49 | convolution fusion | flops 26214400 | bytes 2646016 | tf_op jit(solution)/shard_map/tvh,vtd->thd/dot_general | solution.py:45
  127.7 0.6 fusion.44
  128.4 13.5 %all-to-all-done.2 = f32[8,32,9,128]{3,1,2,0:T(8,128)} async-done(((f32[8,32,9,128]{3,1,2,0:T(8,128)}), f32[8,32,9,128]{3,1,2,0:T(8,128)}, u32[]{:S(2)}, u32[]{:S(2)}) %all-to-all-start.2) | async-done | bytes 1179680 | tf_op jit(solution)/shard_map/all_to_all | solution.py:126
  141.8 1.4 reduce_sum.61
  143.2 0.8 copy.111
  144.0 5.8 %all-to-all-start.3 = ((f32[32,9,128]{2,1,0:T(8,128)}), f32[32,9,128]{2,1,0:T(8,128)S(1)}, u32[]{:S(2)}, u32[]{:S(2)}) async-start(f32[32,9,128]{2,1,0:T(8,128)} %copy.111), calls=%async_computation.3 | async-start | bytes 524288 | tf_op jit(solution)/shard_map/all_to_all | solution.py:127
  149.8 0.7 fusion.31
  150.7 2.6 %fusion.32 = bf16[16,1024]{1,0:T(8,128)(2,1)} fusion(bf16[16,1024]{1,0:T(8,128)(2,1)S(1)} %reshape.70, bf16[2,1024,1024]{2,1,0:T(8,128)(2,1)} %all-gather.2.cloned.1.call-done), kind=kOutput, calls=%fused_computation.42 | convolution fusion | flops 33570816 | bytes 2162688 | tf_op jit(solution)/shard_map/dot_general | solution.py:96
  153.3 8.6 %all-to-all-done.3 = f32[32,9,128]{2,1,0:T(8,128)S(1)} async-done(((f32[32,9,128]{2,1,0:T(8,128)}), f32[32,9,128]{2,1,0:T(8,128)S(1)}, u32[]{:S(2)}, u32[]{:S(2)}) %all-to-all-start.3) | async-done | bytes 147488 | tf_op jit(solution)/shard_map/all_to_all | solution.py:127
  161.8 0.6 reduce_sum.62
  (38 shorter events, 1.7 us)
Async XLA Ops:
  7.2 25.7 %copy-start = (bf16[48,4,1024]{2,1,0:T(4,128)(2,1)S(1)}, bf16[48,4,1024]{2,1,0:T(4,128)(2,1)}, u32[]{:S(2)}) copy-start(bf16[48,4,1024]{2,1,0:T(4,128)(2,1)} %param.11) | copy-start | bytes 1179652
  7.2 87.5 %all-gather.2.cloned.1.call-start = ((), (), s32[]{:S(2)}) async-start(), calls=%async_computation.4 | async-start | bytes 4325376 | tf_op jit(solution)/shard_map/all_gather | solution.py:72
  10.5 9.8 %all-to-all-start.1 = ((bf16[8,2,288]{2,1,0:T(2,128)(2,1)}), bf16[8,2,288]{2,1,0:T(2,128)(2,1)S(1)}, u32[]{:S(2)}, u32[]{:S(2)}) async-start(bf16[8,2,288]{2,1,0:T(2,128)(2,1)} %reshape.94), calls=%async_computation.1 | async-start | bytes 24576 | tf_op jit(solution)/shard_map/all_to_all | solution.py:76
  20.3 20.7 %all-to-all-start = ((f32[32,1,512]{2,1,0:T(1,128)}), f32[32,1,512]{2,1,0:T(1,128)S(1)}, u32[]{:S(2)}, u32[]{:S(2)}) async-start(f32[32,1,512]{2,1,0:T(1,128)} %reshape.96), calls=%async_computation | async-start | bytes 131072 | tf_op jit(solution)/shard_map/all_to_all | solution.py:70
  35.8 9.0 %copy-start.1 = (bf16[48,16,1024]{2,1,0:T(8,128)(2,1)}, bf16[48,16,1024]{2,1,0:T(8,128)(2,1)S(1)}, u32[]{:S(2)}) copy-start(bf16[48,16,1024]{2,1,0:T(8,128)(2,1)S(1)} %get-tuple-element.13) | copy-start | bytes 4718596
  44.9 49.8 %copy-start.4 = (bf16[16,48,80]{1,2,0:T(8,128)(2,1)}, bf16[16,48,80]{1,2,0:T(8,128)(2,1)S(1)}, u32[]{:S(2)}) copy-start(bf16[16,48,80]{1,2,0:T(8,128)(2,1)S(1)} %constant_dynamic-update-slice_fusion.2) | copy-start | bytes 368644
  97.8 2.9 %copy-start.6 = (bf16[16,1024]{1,0:T(8,128)(2,1)S(1)}, bf16[16,1024]{1,0:T(8,128)(2,1)}, u32[]{:S(2)}) copy-start(bf16[16,1024]{1,0:T(8,128)(2,1)} %param.17) | copy-start | bytes 98308
  103.5 1.4 copy-start.2
  104.9 1.5 copy-start.5
  109.3 1.9 %copy-start.3 = (f32[48,16,1024]{2,1,0:T(8,128)S(1)}, f32[48,16,1024]{2,1,0:T(8,128)}, u32[]{:S(2)}) copy-start(f32[48,16,1024]{2,1,0:T(8,128)} %get-tuple-element.14) | copy-start | bytes 9437188
  120.1 21.7 %all-to-all-start.2 = ((f32[8,32,9,128]{3,1,2,0:T(8,128)}), f32[8,32,9,128]{3,1,2,0:T(8,128)}, u32[]{:S(2)}, u32[]{:S(2)}) async-start(f32[8,32,9,128]{3,1,2,0:T(8,128)} %select_bitcast_fusion), calls=%async_computation.2 | async-start | bytes 2359296 | tf_op jit(solution)/shard_map/all_to_all | solution.py:126
  144.0 17.8 %all-to-all-start.3 = ((f32[32,9,128]{2,1,0:T(8,128)}), f32[32,9,128]{2,1,0:T(8,128)S(1)}, u32[]{:S(2)}, u32[]{:S(2)}) async-start(f32[32,9,128]{2,1,0:T(8,128)} %copy.111), calls=%async_computation.3 | async-start | bytes 524288 | tf_op jit(solution)/shard_map/all_to_all | solution.py:127
Sparse Core Ops, SparseCore 0:
  10.6 84.0 all-gather.1

commit v4 on v3

--- a/solution.py
+++ b/solution.py
@@ -78,6 +78,7 @@
     pixels = jnp.take(slot_pixels, live_slot, axis=0)
     pre_act = ein("vpt,vpd->vtd", pixels, patch_weight) + var_embed.astype(f32)[:, None, :]
     embedded = gelu_exact(pre_act).astype(bf16)
+    slope = lax.optimization_barrier(gelu_slope(pre_act))
 
     raw_scores = (ein("vtd,dh->tvh", embedded, wq_hi) + ein("vtd,dh->tvh", embedded, wq_lo)) / math.sqrt(HD)
     squashed = jnp.tanh(raw_scores / score_cap)
@@ -94,9 +95,9 @@
         .reshape(tok_count, width)
     )
     mixed_out = jnp.dot(pooled, out_matrix, preferred_element_type=f32).astype(bf16)
-    contract = (((1,), (1,)), ((), ()))
+    cot_t = lax.optimization_barrier(cotangent.T)
     grad_pooled = (
-        lax.dot_general(out_matrix, cotangent, contract, preferred_element_type=f32)
+        jnp.dot(out_matrix, cot_t, preferred_element_type=f32)
         .T.astype(bf16)
         .reshape(tok_count, H, HD)
     )
@@ -113,7 +114,7 @@
         [spread_hi, spread_lo, jnp.broadcast_to(wq_t[None], (tok_count,) + wq_t.shape)], axis=1
     )
     grad_embed = ein("tvk,tkd->vtd", left, right).astype(bf16)
-    grad_pre = grad_embed.astype(f32) * gelu_slope(pre_act)
+    grad_pre = grad_embed.astype(f32) * slope
     partial = jnp.einsum(
         "vpt,vtd->vpd", pixels.astype(f32), grad_pre, precision=lax.Precision.HIGHEST
     ).reshape(var_total, pixels_per * width)
@@ -122,9 +123,9 @@
     cols = partial.shape[1] // n_tok
     safe = jnp.clip(slot_var, 0, var_total - 1)
     slot_rows = jnp.where((slot_var >= 0)[:, None], jnp.take(partial, safe, axis=0), 0.0)
-    blocks = slot_rows.reshape(n_var, local_slots, n_tok, cols).transpose(0, 2, 1, 3)
+    blocks = slot_rows.reshape(n_var, local_slots, n_tok, cols)
     by_var = lax.all_to_all(blocks, "var", 0, 0, tiled=True).sum(axis=0)
-    by_tok = lax.all_to_all(by_var, "tok", 0, 0, tiled=True).sum(axis=0)
+    by_tok = lax.all_to_all(by_var.transpose(1, 0, 2), "tok", 0, 0, tiled=True).sum(axis=0)
     del slots
     return (mixed_out, by_tok)
 

time: 170 us -> 169 us (level)
  waiting for transfers between devices: 77 us -> 75 us
    dot_general x9, matrix products: 12 us -> 14 us  [ein(): return jnp.einsum(spec, a, b, preferred_element_type=f32)]
    dot_general x1, matrix products: 3.76 us -> 1.99 us  [body(): jnp.einsum('vpt,vtd->vpd', pixels.astype(f32), grad_pre, precision=lax.Pr...]
    unnamed x23 -> x19, local copies, waits for them, and re-layouts: 6.81 us -> 6.38 us
  transfers between devices with their start and end apart: 5 -> 5, of which waited for: 4 -> 4; matrix products, arithmetic and copies ran while one was open for 13% -> 15% of each run, Pallas kernels for 0% -> 0%
where the time goes in v4:
time: 169 us; the launch traced here: 168 us
  waiting for transfers between devices  75 us (44%)
  starting transfers between devices  25.9 us (15%)
  matrix products  20.8 us (12%)
  local copies, waits for them, and re-layouts  19.9 us (12%)
  between operations  14.3 us (8%)
  other arithmetic  12.2 us (7%)
    all_gather x1, waiting for transfers between devices, body(): lax.all_gather(jnp.stack([value_weight, out_weight]), 'tok', axis=1, tile...  48.5 us
    dot_general x9, matrix products, ein(): return jnp.einsum(spec, a, b, preferred_element_type=f32)  14 us
    all_to_all x1, waiting for transfers between devices, body(): by_var = lax.all_to_all(blocks, 'var', 0, 0, tiled=True).sum(axis=0)  13.5 us
    all_to_all x1, starting transfers between devices, body(): lax.all_to_all(wq_copies, 'tok', 0, 0, tiled=True).reshape(n_tok * rows, H)  11.2 us
    all_to_all x1, waiting for transfers between devices, body(): lax.all_to_all(by_var.transpose(1, 0, 2), 'tok', 0, 0, tiled=True)  8.57 us
    unnamed x19, local copies, waits for them, and re-layouts  6.38 us
    slice x2, local copies, waits for them, and re-layouts, body(): value_matrix = full[0]  6 us
    all_to_all x1, starting transfers between devices, body(): lax.all_to_all(by_var.transpose(1, 0, 2), 'tok', 0, 0, tiled=True)  5.81 us
  transfers between devices with their start and end apart: 5, of which 4 were waited for; matrix products, arithmetic and copies ran while one was open for 15% of the time, Pallas kernels for 0%

profile of v4, /device:TPU:32, one launch (start us, length us, event | category | flops | bytes accessed | tf_op | source)
XLA Modules:
  0.0 168.0 jit_solution(15226111260651127036)
XLA Ops:
  7.2 1.6 pad_maximum_fusion.1
  8.8 0.9 copy.95
  9.7 0.8 reshape.94
  10.5 4.5 %all-to-all-start.1 = ((bf16[8,2,288]{2,1,0:T(2,128)(2,1)}), bf16[8,2,288]{2,1,0:T(2,128)(2,1)S(1)}, u32[]{:S(2)}, u32[]{:S(2)}) async-start(bf16[8,2,288]{2,1,0:T(2,128)(2,1)} %reshape.94), calls=%async_computation.1 | async-start | bytes 24576 | tf_op jit(solution)/shard_map/all_to_all | solution.py:76
  15.0 1.0 reshape.73
  15.9 0.8 reshape.74
  16.9 0.8 select_reduce_fusion
  17.7 0.7 compare_and_fusion
  18.4 0.9 convert_element_type.92
  19.3 0.8 reshape.96
  20.3 11.2 %all-to-all-start = ((f32[32,1,512]{2,1,0:T(1,128)}), f32[32,1,512]{2,1,0:T(1,128)S(1)}, u32[]{:S(2)}, u32[]{:S(2)}) async-start(f32[32,1,512]{2,1,0:T(1,128)} %reshape.96), calls=%async_computation | async-start | bytes 131072 | tf_op jit(solution)/shard_map/all_to_all | solution.py:70
  31.5 0.3 reshape.95
  32.2 0.6 gather_fusion
  32.8 3.7 %fusion.4 = (f32[48,16,1024]{2,1,0:T(8,128)}, bf16[48,16,1024]{2,1,0:T(8,128)(2,1)S(1)}) fusion(f32[48,1024]{1,0:T(8,128)S(1)} %convert_element_type.92, bf16[48,4,1024]{2,1,0:T(4,128)(2,1)S(1)} %copy-done, bf16[48,4,16]{2,1,0:T(4,128)(2,1)S(1)} %gather_fusion, pred[48]{0:T(512)(128)(4,1)S(1)} %compare_and_fusion.1), kind=kOutput, calls=%fused_computation.7 | convolution fusion | flops 15731712 | bytes 5314608 | tf_op jit(solution)/shard_map/vpt,vpd->vtd/dot_general | solution.py:45
  36.6 4.4 %all-to-all-done = f32[32,1,512]{2,1,0:T(1,128)S(1)} async-done(((f32[32,1,512]{2,1,0:T(1,128)}), f32[32,1,512]{2,1,0:T(1,128)S(1)}, u32[]{:S(2)}, u32[]{:S(2)}) %all-to-all-start) | async-done | bytes 65568 | tf_op jit(solution)/shard_map/all_to_all | solution.py:70
  41.0 0.5 broadcast.109
  41.5 0.8 reduce
  42.7 1.0 fusion.32
  43.6 1.1 bitcast_reduce_fusion
  44.8 0.8 constant_dynamic-update-slice_fusion.3
  45.5 0.6 constant_dynamic-update-slice_fusion.2
  46.2 48.5 %all-gather.2.cloned.1.call-done = bf16[2,1024,1024]{2,1,0:T(8,128)(2,1)} async-done(((bf16[2,32,1024]{2,1,0:T(8,128)(2,1)}), bf16[2,1024,1024]{2,1,0:T(8,128)(2,1)}) %all-gather.2.cloned.1.call-update) | async-done | bytes 4194320 | tf_op jit(solution)/shard_map/all_gather | solution.py:72
  94.7 3.1 %slice.20 = bf16[1,1024,1024]{2,1,0:T(8,128)(2,1)} slice(bf16[2,1024,1024]{2,1,0:T(8,128)(2,1)} %all-gather.2.cloned.1.call-done), slice={[0:1], [0:1024], [0:1024]} | slice | bytes 4194304 | tf_op jit(solution)/shard_map/slice | solution.py:73
  97.8 2.9 %copy.92 = bf16[1,1024,1024]{1,2,0:T(8,128)(2,1)S(1)} copy(bf16[1,1024,1024]{2,1,0:T(8,128)(2,1)} %slice.20) | data formatting | bytes 4194304 | tf_op jit(solution)/shard_map/slice | solution.py:73
  100.7 2.2 %fusion.25 = bf16[16,1024]{1,0:T(8,128)(2,1)S(1)} fusion(bf16[1024,16]{0,1:T(8,128)(2,1)S(1)} %bitcast.98, bf16[2,1024,1024]{2,1,0:T(8,128)(2,1)} %all-gather.2.cloned.1.call-done), kind=kOutput, calls=%fused_computation.37 | convolution fusion | flops 33570816 | bytes 2162688 | tf_op jit(solution)/shard_map/dot_general | solution.py:100
  103.1 0.4 subtract_convert_fusion
  104.2 0.7 copy-done.2
  104.9 1.5 fusion.26
  106.3 1.9 %constant_dynamic-update-slice_fusion.1 = (bf16[16,48,80]{1,2,0:T(8,128)(2,1)}, f32[16,48,16]{1,2,0:T(8,128)S(1)}) fusion(bf16[16,48,80]{1,2,0:T(8,128)(2,1)} %constant_dynamic-update-slice_fusion.2, f32[16,48,16]{1,0,2:T(8,128)S(1)} %get-tuple-element.16, f32[16,48,32]{1,2,0:T(8,128)S(1)} %fusion.26, f32[16,16]{1,0:T(8,128)S(1)} %get-tuple-element.15), kind=kOutput, calls=%fused_computation.72 | output fusion | flops 172335 | bytes 917504 | tf_op jit(solution)/shard_map/sub | solution.py:108
  108.2 0.6 constant_dynamic-update-slice_fusion
  108.9 0.6 fusion.38
  109.7 1.8 %fusion.7 = bf16[16,1024,48]{1,2,0:T(8,128)(2,1)S(1)} fusion(bf16[16,48,80]{1,2,0:T(8,128)(2,1)} %fusion.38, bf16[16,48,1024]{2,1,0:T(8,128)(2,1)S(1)} %broadcast_in_dim.79, bf16[16,16,1024]{2,1,0:T(8,128)(2,1)S(1)} %copy.106, bf16[16,16,1024]{2,1,0:T(8,128)(2,1)S(1)} %copy.105), kind=kOutput, calls=%fused_computation.14 | convolution fusion | flops 133693440 | bytes 4317184 | tf_op jit(solution)/shard_map/tvk,tkd->vtd/dot_general | solution.py:45
  111.7 2.0 %fusion.5 = f32[48,4,1024]{2,1,0:T(4,128)S(1)} fusion(f32[48,16,1024]{2,1,0:T(8,128)S(1)} %copy-done.3, bf16[16,1024,48]{1,2,0:T(8,128)(2,1)S(1)} %fusion.7, bf16[48,4,16]{2,1,0:T(4,128)(2,1)S(1)} %gather_fusion, pred[48]{0:T(512)(128)(4,1)S(1)} %compare_and_fusion.1), kind=kOutput, calls=%fused_computation.9 | convolution fusion | flops 39324672 | bytes 5511216 | tf_op jit(solution)/shard_map/vpt,vtd->vpd/dot_general | solution.py:118
  113.7 0.5 copy.114
  114.2 1.9 %gather_fusion.1 = f32[72,4096]{1,0:T(8,128)} fusion(f32[48,4096]{1,0:T(8,128)S(1)} %bitcast.83, s32[1024]{0:T(1024)S(1)} %get-tuple-element.19), kind=kCustom, calls=%fused_computation.1 | custom fusion | bytes 2359584 | tf_op jit(solution)/shard_map/jit(_take)/gather | solution.py:125
  116.1 1.5 copy.115
  117.6 1.3 select_select_fusion
  118.9 4.4 %all-to-all-start.2 = ((f32[8,9,32,128]{3,2,1,0:T(8,128)}), f32[8,9,32,128]{3,2,1,0:T(8,128)}, u32[]{:S(2)}, u32[]{:S(2)}) async-start(f32[8,9,32,128]{3,2,1,0:T(8,128)} %select_select_fusion), calls=%async_computation.2 | async-start | bytes 2359296 | tf_op jit(solution)/shard_map/all_to_all | solution.py:127
  123.3 3.2 %subtract_convert_fusion.1 = (bf16[16,16,1024]{2,1,0:T(8,128)(2,1)S(1)}, bf16[16,16,1024]{2,1,0:T(8,128)(2,1)S(1)}) fusion(bf16[16,48,16]{1,2,0:T(8,128)(2,1)S(1)} %get-tuple-element.7, bf16[48,16,1024]{2,1,0:T(8,128)(2,1)} %copy-done.1), kind=kOutput, calls=%fused_computation.42 | convolution fusion | flops 26214400 | bytes 2646016 | tf_op jit(solution)/shard_map/tvh,vtd->thd/dot_general | solution.py:45
  126.5 0.6 fusion.35
  127.1 13.5 %all-to-all-done.2 = f32[8,9,32,128]{3,2,1,0:T(8,128)} async-done(((f32[8,9,32,128]{3,2,1,0:T(8,128)}), f32[8,9,32,128]{3,2,1,0:T(8,128)}, u32[]{:S(2)}, u32[]{:S(2)}) %all-to-all-start.2) | async-done | bytes 1179680 | tf_op jit(solution)/shard_map/all_to_all | solution.py:127
  140.6 1.4 reduce_sum.61
  142.0 0.8 copy.111
  142.8 5.8 %all-to-all-start.3 = ((f32[32,9,128]{2,1,0:T(8,128)}), f32[32,9,128]{2,1,0:T(8,128)S(1)}, u32[]{:S(2)}, u32[]{:S(2)}) async-start(f32[32,9,128]{2,1,0:T(8,128)} %copy.111), calls=%async_computation.3 | async-start | bytes 524288 | tf_op jit(solution)/shard_map/all_to_all | solution.py:128
  148.6 0.7 fusion.22
  149.4 2.6 %fusion.23 = bf16[16,1024]{1,0:T(8,128)(2,1)} fusion(bf16[16,1024]{1,0:T(8,128)(2,1)S(1)} %reshape.70, bf16[2,1024,1024]{2,1,0:T(8,128)(2,1)} %all-gather.2.cloned.1.call-done), kind=kOutput, calls=%fused_computation.35 | convolution fusion | flops 33570816 | bytes 2162688 | tf_op jit(solution)/shard_map/dot_general | solution.py:97
  152.0 8.6 %all-to-all-done.3 = f32[32,9,128]{2,1,0:T(8,128)S(1)} async-done(((f32[32,9,128]{2,1,0:T(8,128)}), f32[32,9,128]{2,1,0:T(8,128)S(1)}, u32[]{:S(2)}, u32[]{:S(2)}) %all-to-all-start.3) | async-done | bytes 147488 | tf_op jit(solution)/shard_map/all_to_all | solution.py:128
  160.6 0.6 reduce_sum.62
  (34 shorter events, 2.6 us)
Async XLA Ops:
  7.2 25.7 %copy-start = (bf16[48,4,1024]{2,1,0:T(4,128)(2,1)S(1)}, bf16[48,4,1024]{2,1,0:T(4,128)(2,1)}, u32[]{:S(2)}) copy-start(bf16[48,4,1024]{2,1,0:T(4,128)(2,1)} %param.11) | copy-start | bytes 1179652
  7.2 87.5 %all-gather.2.cloned.1.call-start = ((), (), s32[]{:S(2)}) async-start(), calls=%async_computation.4 | async-start | bytes 4325376 | tf_op jit(solution)/shard_map/all_gather | solution.py:72
  10.5 9.8 %all-to-all-start.1 = ((bf16[8,2,288]{2,1,0:T(2,128)(2,1)}), bf16[8,2,288]{2,1,0:T(2,128)(2,1)S(1)}, u32[]{:S(2)}, u32[]{:S(2)}) async-start(bf16[8,2,288]{2,1,0:T(2,128)(2,1)} %reshape.94), calls=%async_computation.1 | async-start | bytes 24576 | tf_op jit(solution)/shard_map/all_to_all | solution.py:76
  20.3 20.7 %all-to-all-start = ((f32[32,1,512]{2,1,0:T(1,128)}), f32[32,1,512]{2,1,0:T(1,128)S(1)}, u32[]{:S(2)}, u32[]{:S(2)}) async-start(f32[32,1,512]{2,1,0:T(1,128)} %reshape.96), calls=%async_computation | async-start | bytes 131072 | tf_op jit(solution)/shard_map/all_to_all | solution.py:70
  36.6 8.2 %copy-start.1 = (bf16[48,16,1024]{2,1,0:T(8,128)(2,1)}, bf16[48,16,1024]{2,1,0:T(8,128)(2,1)S(1)}, u32[]{:S(2)}) copy-start(bf16[48,16,1024]{2,1,0:T(8,128)(2,1)S(1)} %get-tuple-element.11) | copy-start | bytes 4718596
  97.8 2.9 %copy-start.4 = (bf16[16,1024]{1,0:T(8,128)(2,1)S(1)}, bf16[16,1024]{1,0:T(8,128)(2,1)}, u32[]{:S(2)}) copy-start(bf16[16,1024]{1,0:T(8,128)(2,1)} %param.17) | copy-start | bytes 98308
  103.5 1.4 copy-start.2
  109.7 2.0 %copy-start.3 = (f32[48,16,1024]{2,1,0:T(8,128)S(1)}, f32[48,16,1024]{2,1,0:T(8,128)}, u32[]{:S(2)}) copy-start(f32[48,16,1024]{2,1,0:T(8,128)} %get-tuple-element.10) | copy-start | bytes 9437188
  118.9 21.7 %all-to-all-start.2 = ((f32[8,9,32,128]{3,2,1,0:T(8,128)}), f32[8,9,32,128]{3,2,1,0:T(8,128)}, u32[]{:S(2)}, u32[]{:S(2)}) async-start(f32[8,9,32,128]{3,2,1,0:T(8,128)} %select_select_fusion), calls=%async_computation.2 | async-start | bytes 2359296 | tf_op jit(solution)/shard_map/all_to_all | solution.py:127
  142.8 17.8 %all-to-all-start.3 = ((f32[32,9,128]{2,1,0:T(8,128)}), f32[32,9,128]{2,1,0:T(8,128)S(1)}, u32[]{:S(2)}, u32[]{:S(2)}) async-start(f32[32,9,128]{2,1,0:T(8,128)} %copy.111), calls=%async_computation.3 | async-start | bytes 524288 | tf_op jit(solution)/shard_map/all_to_all | solution.py:128
Sparse Core Ops, SparseCore 0:
  10.6 84.0 all-gather.1

commit v5 on v4

--- a/solution.py
+++ b/solution.py
@@ -86,11 +86,13 @@
     attn_f32 = exp_scores / jnp.sum(exp_scores, axis=1, keepdims=True)
     attn_bf = attn_f32.astype(bf16)
 
-    value_heads = value_matrix.reshape(width, H, HD)
+    same_head = jnp.arange(H)[:, None] == jnp.arange(H)[None, :]
     mixed_in = ein("tvh,vtd->thd", attn_bf, embedded)
     mix_hi, mix_lo = split(mixed_in)
+    rows_both = jnp.concatenate([mix_hi, mix_lo], axis=0).reshape(2 * tok_count * H, width)
+    all_heads = jnp.dot(rows_both, value_matrix, preferred_element_type=f32).reshape(2, tok_count, H, H, HD)
     pooled = (
-        (ein("thd,dhj->thj", mix_hi, value_heads) + ein("thd,dhj->thj", mix_lo, value_heads))
+        jnp.sum(jnp.where(same_head[None, None, :, :, None], all_heads, 0.0), axis=(0, 3))
         .astype(bf16)
         .reshape(tok_count, width)
     )
@@ -101,7 +103,9 @@
         .T.astype(bf16)
         .reshape(tok_count, H, HD)
     )
-    spread = ein("thj,dhj->thd", grad_pooled, value_heads)
+    by_head = jnp.where(same_head[:, None, None, :], grad_pooled.transpose(1, 2, 0)[:, :, :, None], 0)
+    spread_t = jnp.dot(value_matrix, by_head.reshape(width, tok_count * H).astype(bf16), preferred_element_type=f32)
+    spread = spread_t.reshape(width, tok_count, H).transpose(1, 2, 0)
     spread_hi, spread_lo = split(spread)
     both = ein("vtd,thd->tvh", embedded, jnp.concatenate([spread_hi, spread_lo], axis=1))
     grad_attn = both[:, :, :H] + both[:, :, H:]

time: 169 us -> 167 us (0.988)
  waiting for transfers between devices: 75 us -> 71.7 us
    slice x2 -> x0, local copies, waits for them, and re-layouts: 6 us -> none  [body(): value_matrix = full[0]]
    dot_general x0 -> x2, matrix products: none -> 5.72 us  [the longest x1 3.21 us: body(): jnp.dot(rows_both, value_matrix, preferred_element_type=f32)]
    dot_general x9 -> x6, matrix products: 14 us -> 9.32 us  [ein(): return jnp.einsum(spec, a, b, preferred_element_type=f32)]
    all_to_all x1, waiting for transfers between devices: 8.57 us -> 5.28 us  [body(): lax.all_to_all(by_var.transpose(1, 0, 2), 'tok', 0, 0, tiled=True)]
    dot_general x0 -> x2, local copies, waits for them, and re-layouts: none -> 2.74 us  [body(): jnp.dot(rows_both, value_matrix, preferred_element_type=f32)]
    unnamed x19 -> x23, local copies, waits for them, and re-layouts: 6.38 us -> 6.4 us
  transfers between devices with their start and end apart: 5 -> 5, of which waited for: 4 -> 4; matrix products, arithmetic and copies ran while one was open for 15% -> 16% of each run, Pallas kernels for 0% -> 0%
where the time goes in v5:
time: 167 us; the launch traced here: 166 us
  waiting for transfers between devices  71.7 us (43%)
  starting transfers between devices  26 us (16%)
  matrix products  21.9 us (13%)
  local copies, waits for them, and re-layouts  19.3 us (12%)
  between operations  14.3 us (9%)
  other arithmetic  12.9 us (8%)
    all_gather x1, waiting for transfers between devices, body(): lax.all_gather(jnp.stack([value_weight, out_weight]), 'tok', axis=1, tile...  49.7 us
    all_to_all x1, waiting for transfers between devices, body(): by_var = lax.all_to_all(blocks, 'var', 0, 0, tiled=True).sum(axis=0)  12.3 us
    all_to_all x1, starting transfers between devices, body(): lax.all_to_all(wq_copies, 'tok', 0, 0, tiled=True).reshape(n_tok * rows, H)  11.2 us
    dot_general x6, matrix products, ein(): return jnp.einsum(spec, a, b, preferred_element_type=f32)  9.32 us
    unnamed x23, local copies, waits for them, and re-layouts  6.4 us
    all_to_all x1, starting transfers between devices, body(): lax.all_to_all(by_var.transpose(1, 0, 2), 'tok', 0, 0, tiled=True)  5.87 us
    all_to_all x1, waiting for transfers between devices, body(): lax.all_to_all(by_var.transpose(1, 0, 2), 'tok', 0, 0, tiled=True)  5.28 us
    all_to_all x1, starting transfers between devices, body(): slot_pixels = lax.all_to_all(patches, 'var', 2, 0, tiled=True)  4.47 us
  transfers between devices with their start and end apart: 5, of which 4 were waited for; matrix products, arithmetic and copies ran while one was open for 16% of the time, Pallas kernels for 0%

profile of v5, /device:TPU:32, one launch (start us, length us, event | category | flops | bytes accessed | tf_op | source)
XLA Modules:
  0.0 166.1 jit_solution(17443449755490527013)
XLA Ops:
  7.2 1.6 pad_maximum_fusion.1
  8.8 0.9 copy.60
  9.7 0.8 reshape.139
  10.5 4.5 %all-to-all-start.1 = ((bf16[8,2,288]{2,1,0:T(2,128)(2,1)}), bf16[8,2,288]{2,1,0:T(2,128)(2,1)S(1)}, u32[]{:S(2)}, u32[]{:S(2)}) async-start(bf16[8,2,288]{2,1,0:T(2,128)(2,1)} %reshape.139), calls=%async_computation.1 | async-start | bytes 24576 | tf_op jit(solution)/shard_map/all_to_all | solution.py:76
  15.0 1.0 reshape.115
  15.9 0.8 reshape.116
  16.9 0.8 select_reduce_fusion.1
  17.7 0.7 compare_and_fusion
  18.4 0.9 convert_element_type.101
  19.3 0.8 reshape.141
  20.3 11.2 %all-to-all-start = ((f32[32,1,512]{2,1,0:T(1,128)}), f32[32,1,512]{2,1,0:T(1,128)S(1)}, u32[]{:S(2)}, u32[]{:S(2)}) async-start(f32[32,1,512]{2,1,0:T(1,128)} %reshape.141), calls=%async_computation | async-start | bytes 131072 | tf_op jit(solution)/shard_map/all_to_all | solution.py:70
  31.5 0.3 reshape.140
  31.9 0.3 copy.74
  32.2 0.6 gather_fusion
  32.9 3.7 %fusion.4 = (f32[48,16,1024]{2,1,0:T(8,128)}, bf16[48,16,1024]{2,1,0:T(8,128)(2,1)S(1)}) fusion(f32[48,1024]{1,0:T(8,128)S(1)} %convert_element_type.101, bf16[48,4,1024]{2,1,0:T(4,128)(2,1)S(1)} %copy-done, bf16[48,4,16]{2,1,0:T(4,128)(2,1)S(1)} %gather_fusion, pred[48]{0:T(512)(128)(4,1)S(1)} %compare_and_fusion.1), kind=kOutput, calls=%fused_computation.8 | convolution fusion | flops 15731712 | bytes 5314608 | tf_op jit(solution)/shard_map/vpt,vpd->vtd/dot_general | solution.py:45
  36.6 4.4 %all-to-all-done = f32[32,1,512]{2,1,0:T(1,128)S(1)} async-done(((f32[32,1,512]{2,1,0:T(1,128)}), f32[32,1,512]{2,1,0:T(1,128)S(1)}, u32[]{:S(2)}, u32[]{:S(2)}) %all-to-all-start) | async-done | bytes 65568 | tf_op jit(solution)/shard_map/all_to_all | solution.py:70
  41.0 0.5 broadcast.125
  41.5 0.8 reduce
  42.7 1.0 fusion.35
  43.7 1.1 bitcast_reduce_fusion
  45.0 49.7 %all-gather.2.cloned.1.call-done = bf16[2,1024,1024]{2,1,0:T(8,128)(2,1)} async-done(((bf16[2,32,1024]{2,1,0:T(8,128)(2,1)}), bf16[2,1024,1024]{2,1,0:T(8,128)(2,1)}) %all-gather.2.cloned.1.call-update) | async-done | bytes 4194320 | tf_op jit(solution)/shard_map/all_gather | solution.py:72
  94.7 2.2 %fusion.26 = bf16[16,1024]{1,0:T(8,128)(2,1)S(1)} fusion(bf16[1024,16]{0,1:T(8,128)(2,1)S(1)} %bitcast.121, bf16[2,1024,1024]{2,1,0:T(8,128)(2,1)} %all-gather.2.cloned.1.call-done), kind=kOutput, calls=%fused_computation.38 | convolution fusion | flops 33570816 | bytes 2162688 | tf_op jit(solution)/shard_map/dot_general | solution.py:102
  97.2 1.5 select_n.58
  98.7 2.5 %subtract_convert_fusion = (bf16[16,16,1024]{2,1,0:T(8,128)(2,1)S(1)}, bf16[16,16,1024]{2,1,0:T(8,128)(2,1)S(1)}) fusion(bf16[16,16,1024]{2,1,0:T(8,128)(2,1)} %bitcast.113, bf16[2,1024,1024]{2,1,0:T(8,128)(2,1)} %all-gather.2.cloned.1.call-done), kind=kOutput, calls=%fused_computation.44 | convolution fusion | flops 537919488 | bytes 3670016 | tf_op jit(solution)/shard_map/dot_general | solution.py:107
  101.2 1.1 fusion.27
  102.3 2.7 %constant_dynamic-update-slice_fusion.1 = (bf16[16,48,80]{1,2,0:T(8,128)(2,1)S(1)}, f32[16,48,16]{1,2,0:T(8,128)S(1)}) fusion(bf16[16,48,80]{1,2,0:T(8,128)(2,1)S(1)} %copy-done.5, f32[16,48,16]{1,0,2:T(8,128)S(1)} %get-tuple-element.16, f32[16,48,32]{1,2,0:T(8,128)S(1)} %fusion.27, f32[16,16]{1,0:T(8,128)S(1)} %get-tuple-element.15), kind=kOutput, calls=%fused_computation.72 | output fusion | flops 172335 | bytes 999424 | tf_op jit(solution)/shard_map/sub | solution.py:112
  105.0 0.2 broadcast_in_dim.121
  105.2 0.6 fusion.7
  105.9 1.2 copy-done.2
  107.1 2.0 %fusion.5 = f32[48,4,1024]{2,1,0:T(4,128)S(1)} fusion(f32[48,16,1024]{2,1,0:T(8,128)S(1)} %copy-done.2, bf16[16,1024,48]{1,2,0:T(8,128)(2,1)S(1)} %fusion.7, bf16[48,4,16]{2,1,0:T(4,128)(2,1)S(1)} %gather_fusion, pred[48]{0:T(512)(128)(4,1)S(1)} %compare_and_fusion.1), kind=kOutput, calls=%fused_computation.10 | convolution fusion | flops 39324672 | bytes 5511216 | tf_op jit(solution)/shard_map/vpt,vtd->vpd/dot_general | solution.py:122
  109.1 0.5 copy.75
  109.6 1.9 %gather_fusion.1 = f32[72,4096]{1,0:T(8,128)} fusion(f32[48,4096]{1,0:T(8,128)S(1)} %bitcast.105, s32[1024]{0:T(1024)S(1)} %pad_clamp_fusion), kind=kCustom, calls=%fused_computation.1 | custom fusion | bytes 2359584 | tf_op jit(solution)/shard_map/jit(_take)/gather | solution.py:129
  111.5 1.5 copy.76
  113.0 1.3 select_select_fusion
  114.3 4.4 %all-to-all-start.2 = ((f32[8,9,32,128]{3,2,1,0:T(8,128)}), f32[8,9,32,128]{3,2,1,0:T(8,128)}, u32[]{:S(2)}, u32[]{:S(2)}) async-start(f32[8,9,32,128]{3,2,1,0:T(8,128)} %select_select_fusion), calls=%async_computation.2 | async-start | bytes 2359296 | tf_op jit(solution)/shard_map/all_to_all | solution.py:131
  118.8 1.8 %subtract_convert_fusion.1 = (bf16[16,16,1024]{2,1,0:T(8,128)(2,1)S(1)}, bf16[16,16,1024]{2,1,0:T(8,128)(2,1)S(1)}) fusion(bf16[16,48,16]{1,2,0:T(8,128)(2,1)S(1)} %get-tuple-element.7, bf16[48,16,1024]{2,1,0:T(8,128)(2,1)S(1)} %get-tuple-element.11), kind=kOutput, calls=%fused_computation.45 | convolution fusion | flops 26214400 | bytes 2646016 | tf_op jit(solution)/shard_map/tvh,vtd->thd/dot_general | solution.py:45
  120.6 0.3 copy-done.1
  120.9 0.2 slice_bitcast_fusion.3
  121.1 2.6 %copy.66 = bf16[1024,1024]{1,0:T(8,128)(2,1)} copy(bf16[1024,1024]{0,1:T(8,128)(2,1)S(1)} %slice_bitcast_fusion.3) | data formatting | bytes 4194304 | tf_op jit(solution)/shard_map/dot_general | solution.py:93
  123.7 12.3 %all-to-all-done.2 = f32[8,9,32,128]{3,2,1,0:T(8,128)} async-done(((f32[8,9,32,128]{3,2,1,0:T(8,128)}), f32[8,9,32,128]{3,2,1,0:T(8,128)}, u32[]{:S(2)}, u32[]{:S(2)}) %all-to-all-start.2) | async-done | bytes 1179680 | tf_op jit(solution)/shard_map/all_to_all | solution.py:131
  136.0 2.0 %reduce_sum.71 = f32[9,32,128]{2,1,0:T(8,128)} reduce(f32[8,9,32,128]{3,2,1,0:T(8,128)} %all-to-all-done.2, f32[]{:T(128)} %constant.17.clone.1), dimensions={0}, to_apply=%region_5.6 | reduce | flops 258048 | bytes 1327108 | tf_op jit(solution)/shard_map/reduce_sum | solution.py:131
  138.1 1.7 %copy.70 = f32[32,9,128]{2,1,0:T(8,128)} copy(f32[32,9,128]{2,0,1:T(8,128)} %bitcast.112) | data formatting | bytes 294912 | tf_op jit(solution)/shard_map/transpose | solution.py:132
  139.8 5.9 %all-to-all-start.3 = ((f32[32,9,128]{2,1,0:T(8,128)}), f32[32,9,128]{2,1,0:T(8,128)}, u32[]{:S(2)}, u32[]{:S(2)}) async-start(f32[32,9,128]{2,1,0:T(8,128)} %copy.70), calls=%async_computation.3 | async-start | bytes 524288 | tf_op jit(solution)/shard_map/all_to_all | solution.py:132
  145.7 3.2 %select_reduce_fusion = bf16[16,16,64]{2,1,0:T(8,128)(2,1)} fusion(pred[16,16]{0,1:T(8,128)(4,1)S(1)} %iota_compare_fusion.1, bf16[2,16,16,1024,1]{3,2,4,1,0:T(8,128)(2,1)S(1)} %bitcast.111, bf16[16,64,1024,1,1]{2,1,0,4,3:T(8,128)(2,1)S(1)} %bitcast.109), kind=kOutput, calls=%fused_computation.4 | convolution fusion | flops 1074774016 | bytes 3178752 | tf_op jit(solution)/shard_map/dot_general | solution.py:93
  148.9 1.0 convert_element_type.110
  149.8 2.6 %fusion.24 = bf16[16,1024]{1,0:T(8,128)(2,1)} fusion(bf16[16,1024]{1,0:T(8,128)(2,1)S(1)} %convert_element_type.110, bf16[2,1024,1024]{2,1,0:T(8,128)(2,1)} %all-gather.2.cloned.1.call-done), kind=kOutput, calls=%fused_computation.36 | convolution fusion | flops 33570816 | bytes 2162688 | tf_op jit(solution)/shard_map/dot_general | solution.py:99
  152.4 5.3 %all-to-all-done.3 = f32[32,9,128]{2,1,0:T(8,128)} async-done(((f32[32,9,128]{2,1,0:T(8,128)}), f32[32,9,128]{2,1,0:T(8,128)}, u32[]{:S(2)}, u32[]{:S(2)}) %all-to-all-start.3) | async-done | bytes 147488 | tf_op jit(solution)/shard_map/all_to_all | solution.py:132
  157.7 1.6 reduce_sum.72
  (38 shorter events, 1.5 us)
Async XLA Ops:
  7.2 25.7 %copy-start = (bf16[48,4,1024]{2,1,0:T(4,128)(2,1)S(1)}, bf16[48,4,1024]{2,1,0:T(4,128)(2,1)}, u32[]{:S(2)}) copy-start(bf16[48,4,1024]{2,1,0:T(4,128)(2,1)} %param.11) | copy-start | bytes 1179652
  7.2 87.5 %all-gather.2.cloned.1.call-start = ((), (), s32[]{:S(2)}) async-start(), calls=%async_computation.4 | async-start | bytes 4325376 | tf_op jit(solution)/shard_map/all_gather | solution.py:72
  10.5 9.8 %all-to-all-start.1 = ((bf16[8,2,288]{2,1,0:T(2,128)(2,1)}), bf16[8,2,288]{2,1,0:T(2,128)(2,1)S(1)}, u32[]{:S(2)}, u32[]{:S(2)}) async-start(bf16[8,2,288]{2,1,0:T(2,128)(2,1)} %reshape.139), calls=%async_computation.1 | async-start | bytes 24576 | tf_op jit(solution)/shard_map/all_to_all | solution.py:76
  20.3 20.7 %all-to-all-start = ((f32[32,1,512]{2,1,0:T(1,128)}), f32[32,1,512]{2,1,0:T(1,128)S(1)}, u32[]{:S(2)}, u32[]{:S(2)}) async-start(f32[32,1,512]{2,1,0:T(1,128)} %reshape.141), calls=%async_computation | async-start | bytes 131072 | tf_op jit(solution)/shard_map/all_to_all | solution.py:70
  42.7 52.0 %copy-start.6 = (bf16[16,1024]{1,0:T(8,128)(2,1)S(1)}, bf16[16,1024]{1,0:T(8,128)(2,1)}, u32[]{:S(2)}) copy-start(bf16[16,1024]{1,0:T(8,128)(2,1)} %param.17) | copy-start | bytes 98308
  44.9 52.1 %copy-start.4 = (bf16[16,48,80]{1,2,0:T(8,128)(2,1)}, bf16[16,48,80]{1,2,0:T(8,128)(2,1)S(1)}, u32[]{:S(2)}) copy-start(bf16[16,48,80]{1,2,0:T(8,128)(2,1)S(1)} %constant_dynamic-update-slice_fusion.2) | copy-start | bytes 368644
  101.2 1.1 copy-start.5
  105.2 1.9 %copy-start.2 = (f32[48,16,1024]{2,1,0:T(8,128)S(1)}, f32[48,16,1024]{2,1,0:T(8,128)}, u32[]{:S(2)}) copy-start(f32[48,16,1024]{2,1,0:T(8,128)} %get-tuple-element.10) | copy-start | bytes 9437188
  114.3 21.7 %all-to-all-start.2 = ((f32[8,9,32,128]{3,2,1,0:T(8,128)}), f32[8,9,32,128]{3,2,1,0:T(8,128)}, u32[]{:S(2)}, u32[]{:S(2)}) async-start(f32[8,9,32,128]{3,2,1,0:T(8,128)} %select_select_fusion), calls=%async_computation.2 | async-start | bytes 2359296 | tf_op jit(solution)/shard_map/all_to_all | solution.py:131
  118.7 2.2 %copy-start.1 = (bf16[2,1024,1024]{2,1,0:T(8,128)(2,1)S(1)}, bf16[2,1024,1024]{2,1,0:T(8,128)(2,1)}, u32[]{:S(2)}) copy-start(bf16[2,1024,1024]{2,1,0:T(8,128)(2,1)} %all-gather.2.cloned.1.call-done) | copy-start | bytes 12582916
  123.7 22.0 %copy-start.3 = (bf16[1024,1024]{1,0:T(8,128)(2,1)S(1)}, bf16[1024,1024]{1,0:T(8,128)(2,1)}, u32[]{:S(2)}) copy-start(bf16[1024,1024]{1,0:T(8,128)(2,1)} %copy.66) | copy-start | bytes 6291460
  139.8 17.9 %all-to-all-start.3 = ((f32[32,9,128]{2,1,0:T(8,128)}), f32[32,9,128]{2,1,0:T(8,128)}, u32[]{:S(2)}, u32[]{:S(2)}) async-start(f32[32,9,128]{2,1,0:T(8,128)} %copy.70), calls=%async_computation.3 | async-start | bytes 524288 | tf_op jit(solution)/shard_map/all_to_all | solution.py:132
Sparse Core Ops, SparseCore 0:
  10.6 84.0 all-gather.1

commit v6 on v5

--- a/solution.py
+++ b/solution.py
@@ -43,6 +43,34 @@
 
 def ein(spec, a, b):
     return jnp.einsum(spec, a, b, preferred_element_type=f32)
+
+
+def ring_steps(block, n, perm_of):
+    forward, backward = block, block
+    behind, ahead = [], []
+    for k in range(1, n // 2 + 1):
+        forward = lax.ppermute(forward, "tok", perm_of(1))
+        behind.append(forward)
+        if k < n - k:
+            backward = lax.ppermute(backward, "tok", perm_of(-1))
+            ahead.append(backward)
+    return jnp.stack([block] + behind + ahead[::-1])
+
+
+def ring_gather(block, n_x, n_z):
+    def along_z(step):
+        return [(x * n_z + z, x * n_z + (z + step) % n_z) for x in range(n_x) for z in range(n_z)]
+
+    def along_x(step):
+        return [(x * n_z + z, ((x + step) % n_x) * n_z + z) for x in range(n_x) for z in range(n_z)]
+
+    me = lax.axis_index("tok")
+    my_z, my_x = me % n_z, me // n_z
+    by_z = ring_steps(block, n_z, along_z)
+    by_z = jnp.take(by_z, (my_z - jnp.arange(n_z)) % n_z, axis=0)
+    by_x = ring_steps(by_z, n_x, along_x)
+    by_x = jnp.take(by_x, (my_x - jnp.arange(n_x)) % n_x, axis=0)
+    return by_x.reshape((n_x * n_z * block.shape[0],) + block.shape[1:])
 
 
 def body(
@@ -58,6 +86,8 @@
     *,
     n_var,
     n_tok,
+    n_tok_x,
+    n_tok_z,
 ):
     var_total, pixels_per, width = patch_weight.shape
     local_slots = patches.shape[0]
@@ -69,9 +99,12 @@
     wq_copies = jnp.broadcast_to(wq_rows[None], (n_tok, rows, H))
     wq_full = lax.all_to_all(wq_copies, "tok", 0, 0, tiled=True).reshape(n_tok * rows, H)
     wq_hi, wq_lo = split(wq_full)
-    full = lax.all_gather(jnp.stack([value_weight, out_weight]), "tok", axis=1, tiled=True)
-    value_matrix = full[0]
-    out_matrix = full[1]
+    core = lax.axis_index("var") % 2
+    mine = jnp.where(core == 0, value_weight, out_weight)
+    gathered = ring_gather(mine, n_tok_x, n_tok_z)
+    other = lax.ppermute(gathered, "var", [(i, i ^ 1) for i in range(n_var)])
+    value_matrix = jnp.where(core == 0, gathered, other)
+    out_matrix = jnp.where(core == 0, other, gathered)
 
     slot_pixels = lax.all_to_all(patches, "var", 2, 0, tiled=True)
     live_slot = live_index(slot_var, var_total)
@@ -134,10 +167,24 @@
     return (mixed_out, by_tok)
 
 
+def inner_ring(mesh, n_tok):
+    try:
+        row = mesh.devices[0]
+        slow = [tuple(d.coords)[0] for d in row]
+        size = next((i for i in range(1, n_tok) if slow[i] != slow[0]), n_tok)
+        if n_tok % size == 0:
+            return size
+    except (AttributeError, TypeError, IndexError):
+        pass
+    return n_tok
+
+
 def solution(mesh):
     import functools
 
-    fn = functools.partial(body, n_var=mesh.shape["var"], n_tok=mesh.shape["tok"])
+    n_tok = mesh.shape["tok"]
+    n_tok_z = inner_ring(mesh, n_tok)
+    fn = functools.partial(body, n_var=mesh.shape["var"], n_tok=n_tok, n_tok_x=n_tok // n_tok_z, n_tok_z=n_tok_z)
     return jax.shard_map(
         fn,
         mesh=mesh,

time: 167 us -> 158 us (0.946)
  waiting for transfers between devices: 71.7 us -> 51.2 us
  between operations: 14.3 us -> 1.2 us
  starting transfers between devices: 26 us -> 37.3 us
  other arithmetic: 12.9 us -> 17.8 us
  local copies, waits for them, and re-layouts: 19.3 us -> 24 us
  matrix products: 21.9 us -> 26 us
    all_gather x1 -> x0, waiting for transfers between devices: 49.7 us -> none  [body(): lax.all_gather(jnp.stack([value_weight, out_weight]), 'tok', axis=1, tile...]
    ppermute x0 -> x11, waiting for transfers between devices: none -> 30.5 us  [the longest x6 29.9 us: ring_steps(): forward = lax.ppermute(forward, 'tok', perm_of(1))]
    ppermute x0 -> x11, starting transfers between devices: none -> 13.2 us  [the longest x6 6.75 us: ring_steps(): forward = lax.ppermute(forward, 'tok', perm_of(1))]
    all_to_all x1, waiting for transfers between devices: 12.3 us -> 7.33 us  [body(): by_var = lax.all_to_all(blocks, 'var', 0, 0, tiled=True).sum(axis=0)]
    all_to_all x1, waiting for transfers between devices: 5.28 us -> 9.36 us  [body(): lax.all_to_all(by_var.transpose(1, 0, 2), 'tok', 0, 0, tiled=True)]
    dot_general x6, matrix products: 9.32 us -> 13.3 us  [ein(): return jnp.einsum(spec, a, b, preferred_element_type=f32)]
    gather x0 -> x2, local copies, waits for them, and re-layouts: none -> 2.85 us  [the longest x1 2.27 us: ring_gather(): by_x = jnp.take(by_x, (my_x - jnp.arange(n_x)) % n_x, axis=0)]
    select_n x0 -> x5, other arithmetic: none -> 2.03 us  [the longest x2 1.78 us: ring_gather(): by_x = jnp.take(by_x, (my_x - jnp.arange(n_x)) % n_x, axis=0)]
  transfers between devices with their start and end apart: 5 -> 15, of which waited for: 4 -> 9; matrix products, arithmetic and copies ran while one was open for 16% -> 26% of each run, Pallas kernels for 0% -> 0%
where the time goes in v6:
time: 158 us
  waiting for transfers between devices  51.2 us (32%)
  starting transfers between devices  37.3 us (24%)
  matrix products  26 us (16%)
  local copies, waits for them, and re-layouts  24 us (15%)
  other arithmetic  17.8 us (11%)
    ppermute x6, waiting for transfers between devices, ring_steps(): forward = lax.ppermute(forward, 'tok', perm_of(1))  29.9 us
    dot_general x6, matrix products, ein(): return jnp.einsum(spec, a, b, preferred_element_type=f32)  13.3 us
    all_to_all x1, starting transfers between devices, body(): lax.all_to_all(wq_copies, 'tok', 0, 0, tiled=True).reshape(n_tok * rows, H)  9.54 us
    all_to_all x1, waiting for transfers between devices, body(): lax.all_to_all(by_var.transpose(1, 0, 2), 'tok', 0, 0, tiled=True)  9.36 us
    all_to_all x1, waiting for transfers between devices, body(): by_var = lax.all_to_all(blocks, 'var', 0, 0, tiled=True).sum(axis=0)  7.33 us
    unnamed x57, local copies, waits for them, and re-layouts  6.9 us
    ppermute x6, starting transfers between devices, ring_steps(): forward = lax.ppermute(forward, 'tok', perm_of(1))  6.75 us
    ppermute x4, starting transfers between devices, ring_steps(): backward = lax.ppermute(backward, 'tok', perm_of(-1))  6.48 us
  transfers between devices with their start and end apart: 15, of which 9 were waited for; matrix products, arithmetic and copies ran while one was open for 26% of the time, Pallas kernels for 0%

profile of v6, /device:TPU:32, one launch (start us, length us, event | category | flops | bytes accessed | tf_op | source)
XLA Modules:
  0.0 157.5 jit_solution(6378815027409704544)
XLA Ops:
  0.7 0.9 bitcast_dynamic-update-slice_fusion.7
  1.6 2.0 %collective-permute-start = (bf16[32,1024]{1,0:T(8,128)(2,1)S(1)}, bf16[32,1024]{1,0:T(8,128)(2,1)S(1)}, u32[]{:S(2)}, u32[]{:S(2)}) collective-permute-start(bf16[32,1024]{1,0:T(8,128)(2,1)S(1)} %get-tuple-element.9), channel_id=1, source_target_pairs={{0,1},{1,2},{2,3},{3,4},{4,5},{5,6},{6,7},{7,0},{8,9},{9,10},{10,1... | collective-permute-start | bytes 196616 | tf_op jit(solution)/shard_map/ppermute | solution.py:52
  3.7 0.9 copy.61
  5.3 4.5 %all-to-all-start.1 = ((bf16[8,2,288]{2,1,0:T(2,128)(2,1)}), bf16[8,2,288]{2,1,0:T(2,128)(2,1)S(1)}, u32[]{:S(2)}, u32[]{:S(2)}) async-start(bf16[8,2,288]{2,1,0:T(2,128)(2,1)} %reshape.267), calls=%async_computation.1 | async-start | bytes 24576 | tf_op jit(solution)/shard_map/all_to_all | solution.py:109
  10.6 1.0 reshape.227
  12.6 2.0 %collective-permute-start.1 = (bf16[32,1024]{1,0:T(8,128)(2,1)S(1)}, bf16[32,1024]{1,0:T(8,128)(2,1)S(1)}, u32[]{:S(2)}, u32[]{:S(2)}) collective-permute-start(bf16[32,1024]{1,0:T(8,128)(2,1)S(1)} %collective-permute-done), channel_id=1, source_target_pairs={{0,1},{1,2},{2,3},{3,4},{4,5},{5,6},{6,7},{7,0},{8,9},{9,10},{10,1... | collective-permute-start | bytes 196616 | tf_op jit(solution)/shard_map/ppermute | solution.py:52
  14.6 2.2 %collective-permute-start.5 = (bf16[32,1024]{1,0:T(8,128)(2,1)S(1)}, bf16[32,1024]{1,0:T(8,128)(2,1)S(1)}, u32[]{:S(2)}, u32[]{:S(2)}) collective-permute-start(bf16[32,1024]{1,0:T(8,128)(2,1)S(1)} %collective-permute-done.4), channel_id=1, source_target_pairs={{0,7},{1,0},{2,1},{3,2},{4,3},{5,4},{6,5},{7,6},{8,15},{9,8},{10,9... | collective-permute-start | bytes 196616 | tf_op jit(solution)/shard_map/ppermute | solution.py:55
  16.8 2.6 %collective-permute-done.1 = bf16[32,1024]{1,0:T(8,128)(2,1)S(1)} collective-permute-done((bf16[32,1024]{1,0:T(8,128)(2,1)S(1)}, bf16[32,1024]{1,0:T(8,128)(2,1)S(1)}, u32[]{:S(2)}, u32[]{:S(2)}) %collective-permute-start.1) | collective-permute-done | bytes 65568 | tf_op jit(solution)/shard_map/ppermute | solution.py:52
  20.2 2.3 %collective-permute-start.6 = (bf16[32,1024]{1,0:T(8,128)(2,1)S(1)}, bf16[32,1024]{1,0:T(8,128)(2,1)S(1)}, u32[]{:S(2)}, u32[]{:S(2)}) collective-permute-start(bf16[32,1024]{1,0:T(8,128)(2,1)S(1)} %collective-permute-done.5), channel_id=1, source_target_pairs={{0,7},{1,0},{2,1},{3,2},{4,3},{5,4},{6,5},{7,6},{8,15},{9,8},{10,9... | collective-permute-start | bytes 196616 | tf_op jit(solution)/shard_map/ppermute | solution.py:55
  22.5 2.1 %collective-permute-done.2 = bf16[32,1024]{1,0:T(8,128)(2,1)S(1)} collective-permute-done((bf16[32,1024]{1,0:T(8,128)(2,1)S(1)}, bf16[32,1024]{1,0:T(8,128)(2,1)S(1)}, u32[]{:S(2)}, u32[]{:S(2)}) %collective-permute-start.2) | collective-permute-done | bytes 65568 | tf_op jit(solution)/shard_map/ppermute | solution.py:52
  24.8 5.4 %collective-permute-done.3 = bf16[32,1024]{1,0:T(8,128)(2,1)S(1)} collective-permute-done((bf16[32,1024]{1,0:T(8,128)(2,1)S(1)}, bf16[32,1024]{1,0:T(8,128)(2,1)S(1)}, u32[]{:S(2)}, u32[]{:S(2)}) %collective-permute-start.3) | collective-permute-done | bytes 65568 | tf_op jit(solution)/shard_map/ppermute | solution.py:52
  30.9 1.6 collective-permute-start.7
  32.5 1.8 %collective-permute-start.9 = (bf16[8,32,1024]{2,1,0:T(8,128)(2,1)S(1)}, bf16[8,32,1024]{2,1,0:T(8,128)(2,1)S(1)}, u32[]{:S(2)}, u32[]{:S(2)}) collective-permute-start(bf16[8,32,1024]{2,1,0:T(8,128)(2,1)S(1)} %broadcast_select_fusion.6), channel_id=1, source_target_pairs={{0,24},{1,25},{2,26},{3,27},{4,28},{5,29},{6,30},{7,31},{8,0},{9,1... | collective-permute-start | bytes 1572872 | tf_op jit(solution)/shard_map/ppermute | solution.py:55
  34.3 9.3 %collective-permute-done.7 = bf16[8,32,1024]{2,1,0:T(8,128)(2,1)S(1)} collective-permute-done((bf16[8,32,1024]{2,1,0:T(8,128)(2,1)S(1)}, bf16[8,32,1024]{2,1,0:T(8,128)(2,1)S(1)}, u32[]{:S(2)}, u32[]{:S(2)}) %collective-permute-start.7) | collective-permute-done | bytes 524320 | tf_op jit(solution)/shard_map/ppermute | solution.py:52
  43.6 0.9 collective-permute-start.8
  44.9 10.5 %collective-permute-done.8 = bf16[8,32,1024]{2,1,0:T(8,128)(2,1)S(1)} collective-permute-done((bf16[8,32,1024]{2,1,0:T(8,128)(2,1)S(1)}, bf16[8,32,1024]{2,1,0:T(8,128)(2,1)S(1)}, u32[]{:S(2)}, u32[]{:S(2)}) %collective-permute-start.8) | collective-permute-done | bytes 524320 | tf_op jit(solution)/shard_map/ppermute | solution.py:52
  55.4 1.6 %pad_maximum_fusion = bf16[4,8,32,1024]{3,2,1,0:T(8,128)(2,1)} fusion(bf16[1,8,32,1024]{3,2,1,0:T(8,128)(2,1)S(1)} %bitcast.133, bf16[1,8,32,1024]{3,2,1,0:T(8,128)(2,1)S(1)} %bitcast.134, bf16[1,8,32,1024]{3,2,1,0:T(8,128)(2,1)S(1)} %bitcast.132, bf16[1,8,32,1024]{3,2,1,0:T(8,128)(2,1)S(1)} %bitcast_select_fusion.1), kind=kLoop, calls=%fused_computation.23 | loop fusion | flops 3145728 | bytes 4194304 | tf_op jit(solution)/shard_map/stack | solution.py:57
  57.0 2.3 %gather_fusion.2 = bf16[4,8,32,1024]{3,2,1,0:T(8,128)(2,1)S(1)} fusion(bf16[4,8,32,1024]{3,2,1,0:T(8,128)(2,1)} %pad_maximum_fusion, s32[1024]{0:T(1024)S(1)} %pad_clamp_fusion.1), kind=kCustom, calls=%fused_computation.2 | custom fusion | bytes 4194320 | tf_op jit(solution)/shard_map/jit(_take)/gather | solution.py:72
  59.3 1.8 %bitcast_select_fusion = bf16[1024,1024]{1,0:T(8,128)(2,1)} fusion(bf16[4,8,32,1024]{3,2,1,0:T(8,128)(2,1)S(1)} %gather_fusion.2, pred[1024]{0:T(1024)(128)(4,1)S(1)} %broadcast_in_dim.142), kind=kLoop, calls=%fused_computation.26 | loop fusion | flops 1048576 | bytes 4195328 | tf_op jit(solution)/shard_map/jit(_take)/select_n | solution.py:72
  63.8 9.5 %all-to-all-start = ((f32[32,1,512]{2,1,0:T(1,128)}), f32[32,1,512]{2,1,0:T(1,128)S(1)}, u32[]{:S(2)}, u32[]{:S(2)}) async-start(f32[32,1,512]{2,1,0:T(1,128)} %reshape.269), calls=%async_computation | async-start | bytes 131072 | tf_op jit(solution)/shard_map/all_to_all | solution.py:100
  74.7 3.8 %fusion.4 = (f32[48,16,1024]{2,1,0:T(8,128)}, bf16[48,16,1024]{2,1,0:T(8,128)(2,1)}) fusion(f32[48,1024]{1,0:T(8,128)S(1)} %convert_element_type.95, bf16[48,4,1024]{2,1,0:T(4,128)(2,1)S(1)} %copy-done, bf16[48,4,16]{2,1,0:T(4,128)(2,1)S(1)} %gather_fusion, pred[48]{0:T(512)(128)(4,1)S(1)} %compare_and_fusion.3), kind=kOutput, calls=%fused_computation.10 | convolution fusion | flops 15731712 | bytes 5314608 | tf_op jit(solution)/shard_map/vpt,vpd->vtd/dot_general | solution.py:45
  78.5 4.0 %all-to-all-done = f32[32,1,512]{2,1,0:T(1,128)S(1)} async-done(((f32[32,1,512]{2,1,0:T(1,128)}), f32[32,1,512]{2,1,0:T(1,128)S(1)}, u32[]{:S(2)}, u32[]{:S(2)}) %all-to-all-start) | async-done | bytes 65568 | tf_op jit(solution)/shard_map/all_to_all | solution.py:100
  83.0 0.8 reduce
  84.2 2.5 %fusion.30 = f32[16,48,16]{1,0,2:T(8,128)S(1)} fusion(bf16[48,16,1024]{2,1,0:T(8,128)(2,1)} %get-tuple-element.13, f32[1024,16]{0,1:T(8,128)S(1)} %reshape.224), kind=kOutput, calls=%fused_computation.52 | convolution fusion | flops 25182208 | bytes 1687552 | tf_op jit(solution)/shard_map/vtd,dh->tvh/dot_general | solution.py:45
  86.7 2.5 %bitcast_reduce_fusion = (f32[16,16]{1,0:T(8,128)S(1)}, f32[16,48,16]{1,0,2:T(8,128)S(1)}) fusion(f32[16,48,16]{1,0,2:T(8,128)S(1)} %fusion.30, bf16[48,16,1024]{2,1,0:T(8,128)(2,1)} %get-tuple-element.13, f32[1024,16]{0,1:T(8,128)S(1)} %reshape.224), kind=kOutput, calls=%fused_computation.60 | convolution fusion | flops 25280256 | bytes 1737728 | tf_op jit(solution)/shard_map/vtd,dh->tvh/dot_general | solution.py:45
  90.7 2.8 %subtract_convert_fusion.1 = (bf16[16,16,1024]{2,1,0:T(8,128)(2,1)}, bf16[16,16,1024]{2,1,0:T(8,128)(2,1)}) fusion(bf16[16,48,16]{1,2,0:T(8,128)(2,1)S(1)} %get-tuple-element.7, bf16[48,16,1024]{2,1,0:T(8,128)(2,1)S(1)} %copy-done.1), kind=kOutput, calls=%fused_computation.46 | convolution fusion | flops 26214400 | bytes 2646016 | tf_op jit(solution)/shard_map/tvh,vtd->thd/dot_general | solution.py:45
  93.5 2.2 %fusion.21 = bf16[16,1024]{1,0:T(8,128)(2,1)S(1)} fusion(bf16[1024,16]{0,1:T(8,128)(2,1)S(1)} %bitcast.137, bf16[1024,1024]{1,0:T(8,128)(2,1)} %collective-permute-done.10, bf16[1024,1024]{1,0:T(8,128)(2,1)} %bitcast_select_fusion, pred[]{:T(512)S(6)} %eq.58), kind=kOutput, calls=%fused_computation.39 | convolution fusion | flops 34619392 | bytes 4259841 | tf_op jit(solution)/shard_map/dot_general | solution.py:135
  96.5 1.0 broadcast_select_fusion.2
  97.5 1.5 select_n.196
  99.1 2.6 %subtract_convert_fusion = (bf16[16,16,1024]{2,1,0:T(8,128)(2,1)S(1)}, bf16[16,16,1024]{2,1,0:T(8,128)(2,1)S(1)}) fusion(bf16[16,16,1024]{2,1,0:T(8,128)(2,1)} %bitcast.128, bf16[1024,1024]{1,0:T(8,128)(2,1)} %bitcast_select_fusion, bf16[1024,1024]{1,0:T(8,128)(2,1)} %collective-permute-done.10, pred[]{:T(512)S(6)} %eq.58), kind=kOutput, calls=%fused_computation.45 | convolution fusion | flops 538968064 | bytes 5767169 | tf_op jit(solution)/shard_map/dot_general | solution.py:140
  101.7 1.1 fusion.22
  102.9 3.0 %constant_dynamic-update-slice_fusion.1 = (bf16[16,48,80]{1,2,0:T(8,128)(2,1)S(1)}, f32[16,48,16]{1,2,0:T(8,128)S(1)}) fusion(bf16[16,48,80]{1,2,0:T(8,128)(2,1)S(1)} %copy-done.14, f32[16,48,16]{1,0,2:T(8,128)S(1)} %copy-done.11, f32[16,48,32]{1,2,0:T(8,128)S(1)} %fusion.22, f32[16,16]{1,0:T(8,128)S(1)} %get-tuple-element.17), kind=kOutput, calls=%fused_computation.82 | output fusion | flops 172335 | bytes 999424 | tf_op jit(solution)/shard_map/sub | solution.py:145
  106.8 1.2 copy-done.3
  108.0 2.0 %fusion.5 = f32[48,4,1024]{2,1,0:T(4,128)S(1)} fusion(f32[48,16,1024]{2,1,0:T(8,128)S(1)} %copy-done.3, bf16[16,1024,48]{1,2,0:T(8,128)(2,1)S(1)} %fusion.7, bf16[48,4,16]{2,1,0:T(4,128)(2,1)S(1)} %copy-done.9, pred[48]{0:T(512)(128)(4,1)S(1)} %copy-done.18), kind=kOutput, calls=%fused_computation.12 | convolution fusion | flops 39324672 | bytes 5511216 | tf_op jit(solution)/shard_map/vpt,vtd->vpd/dot_general | solution.py:155
  110.5 2.1 %gather_fusion.3 = f32[72,4096]{1,0:T(8,128)} fusion(f32[48,4096]{1,0:T(8,128)S(1)} %bitcast.120, s32[1024]{0:T(1024)} %pad_clamp_fusion), kind=kCustom, calls=%fused_computation.3 | custom fusion | bytes 2359584 | tf_op jit(solution)/shard_map/jit(_take)/gather | solution.py:162
  112.5 1.5 copy.77
  114.1 1.3 select_select_fusion
  115.3 4.2 %all-to-all-start.2 = ((f32[8,9,32,128]{3,2,1,0:T(8,128)}), f32[8,9,32,128]{3,2,1,0:T(8,128)}, u32[]{:S(2)}, u32[]{:S(2)}) async-start(f32[8,9,32,128]{3,2,1,0:T(8,128)} %select_select_fusion), calls=%async_computation.2 | async-start | bytes 2359296 | tf_op jit(solution)/shard_map/all_to_all | solution.py:164
  119.6 1.1 pad_maximum_fusion.1
  120.7 1.8 %fusion.32 = bf16[1024,1024]{0,1:T(8,128)(2,1)} fusion(bf16[1024,1024]{1,0:T(8,128)(2,1)} %collective-permute-done.10, pred[]{:T(512)S(6)} %eq.58, bf16[4,8,32,1024]{3,2,1,0:T(8,128)(2,1)S(1)} %gather_fusion.2, pred[1024]{0:T(1024)(128)(4,1)S(1)} %broadcast_in_dim.142), kind=kLoop, calls=%fused_computation.54 | loop fusion | flops 2097152 | bytes 6292481 | tf_op jit(solution)/shard_map/dot_general | solution.py:126
  122.5 2.9 %copy.67 = bf16[1024,1024]{1,0:T(8,128)(2,1)S(1)} copy(bf16[1024,1024]{0,1:T(8,128)(2,1)} %fusion.32) | data formatting | bytes 4194304 | tf_op jit(solution)/shard_map/dot_general | solution.py:126
  125.4 3.2 %select_reduce_fusion = bf16[16,16,64]{2,1,0:T(8,128)(2,1)} fusion(pred[16,16]{0,1:T(8,128)(4,1)S(1)} %iota_compare_fusion.1, bf16[2,16,16,1024,1]{3,2,4,1,0:T(8,128)(2,1)S(1)} %bitcast.126, bf16[16,64,1024,1,1]{2,1,0,4,3:T(8,128)(2,1)S(1)} %bitcast.124), kind=kOutput, calls=%fused_computation.6 | convolution fusion | flops 1074774016 | bytes 3178752 | tf_op jit(solution)/shard_map/dot_general | solution.py:126
  128.6 1.0 convert_element_type.104
  129.6 7.3 %all-to-all-done.2 = f32[8,9,32,128]{3,2,1,0:T(8,128)} async-done(((f32[8,9,32,128]{3,2,1,0:T(8,128)}), f32[8,9,32,128]{3,2,1,0:T(8,128)}, u32[]{:S(2)}, u32[]{:S(2)}) %all-to-all-start.2) | async-done | bytes 1179680 | tf_op jit(solution)/shard_map/all_to_all | solution.py:164
  136.9 1.4 reduce_sum.71
  139.1 5.8 %all-to-all-start.3 = ((f32[32,9,128]{2,1,0:T(8,128)}), f32[32,9,128]{2,1,0:T(8,128)S(1)}, u32[]{:S(2)}, u32[]{:S(2)}) async-start(f32[32,9,128]{2,1,0:T(8,128)} %copy.71), calls=%async_computation.3 | async-start | bytes 524288 | tf_op jit(solution)/shard_map/all_to_all | solution.py:165
  144.9 2.6 %convolution_convert_fusion.1 = bf16[16,1024]{1,0:T(8,128)(2,1)} fusion(bf16[16,1024]{1,0:T(8,128)(2,1)S(1)} %convert_element_type.104, bf16[1024,1024]{1,0:T(8,128)(2,1)} %collective-permute-done.10, bf16[1024,1024]{1,0:T(8,128)(2,1)} %bitcast_select_fusion, pred[]{:T(512)S(6)} %eq.58), kind=kOutput, calls=%fused_computation.38 | convolution fusion | flops 34619392 | bytes 4259841 | tf_op jit(solution)/shard_map/dot_general | solution.py:132
  147.5 9.4 %all-to-all-done.3 = f32[32,9,128]{2,1,0:T(8,128)S(1)} async-done(((f32[32,9,128]{2,1,0:T(8,128)}), f32[32,9,128]{2,1,0:T(8,128)S(1)}, u32[]{:S(2)}, u32[]{:S(2)}) %all-to-all-start.3) | async-done | bytes 147488 | tf_op jit(solution)/shard_map/all_to_all | solution.py:165
  (106 shorter events, 14.5 us)
Async XLA Ops:
  0.6 74.1 %copy-start = (bf16[48,4,1024]{2,1,0:T(4,128)(2,1)S(1)}, bf16[48,4,1024]{2,1,0:T(4,128)(2,1)}, u32[]{:S(2)}) copy-start(bf16[48,4,1024]{2,1,0:T(4,128)(2,1)} %param.11) | copy-start | bytes 1179652
  0.7 31.8 %copy-start.19 = (s32[72]{0:T(128)S(1)}, s32[72]{0:T(128)}, u32[]{:S(2)}) copy-start(s32[72]{0:T(128)} %param.10) | copy-start | bytes 868
  1.6 11.0 %collective-permute-start = (bf16[32,1024]{1,0:T(8,128)(2,1)S(1)}, bf16[32,1024]{1,0:T(8,128)(2,1)S(1)}, u32[]{:S(2)}, u32[]{:S(2)}) collective-permute-start(bf16[32,1024]{1,0:T(8,128)(2,1)S(1)} %get-tuple-element.9), channel_id=1, source_target_pairs={{0,1},{1,2},{2,3},{3,4},{4,5},{5,6},{6,7},{7,0},{8,9},{9,10},{10,1... | collective-permute-start | bytes 196616 | tf_op jit(solution)/shard_map/ppermute | solution.py:52
  3.6 11.0 %collective-permute-start.4 = (bf16[32,1024]{1,0:T(8,128)(2,1)S(1)}, bf16[32,1024]{1,0:T(8,128)(2,1)S(1)}, u32[]{:S(2)}, u32[]{:S(2)}) collective-permute-start(bf16[32,1024]{1,0:T(8,128)(2,1)S(1)} %get-tuple-element.9), channel_id=1, source_target_pairs={{0,7},{1,0},{2,1},{3,2},{4,3},{5,4},{6,5},{7,6},{8,15},{9,8},{10,9... | collective-permute-start | bytes 196616 | tf_op jit(solution)/shard_map/ppermute | solution.py:55
  5.3 58.5 %all-to-all-start.1 = ((bf16[8,2,288]{2,1,0:T(2,128)(2,1)}), bf16[8,2,288]{2,1,0:T(2,128)(2,1)S(1)}, u32[]{:S(2)}, u32[]{:S(2)}) async-start(bf16[8,2,288]{2,1,0:T(2,128)(2,1)} %reshape.267), calls=%async_computation.1 | async-start | bytes 24576 | tf_op jit(solution)/shard_map/all_to_all | solution.py:109
  12.6 6.9 %collective-permute-start.1 = (bf16[32,1024]{1,0:T(8,128)(2,1)S(1)}, bf16[32,1024]{1,0:T(8,128)(2,1)S(1)}, u32[]{:S(2)}, u32[]{:S(2)}) collective-permute-start(bf16[32,1024]{1,0:T(8,128)(2,1)S(1)} %collective-permute-done), channel_id=1, source_target_pairs={{0,1},{1,2},{2,3},{3,4},{4,5},{5,6},{6,7},{7,0},{8,9},{9,10},{10,1... | collective-permute-start | bytes 196616 | tf_op jit(solution)/shard_map/ppermute | solution.py:52
  14.6 5.6 %collective-permute-start.5 = (bf16[32,1024]{1,0:T(8,128)(2,1)S(1)}, bf16[32,1024]{1,0:T(8,128)(2,1)S(1)}, u32[]{:S(2)}, u32[]{:S(2)}) collective-permute-start(bf16[32,1024]{1,0:T(8,128)(2,1)S(1)} %collective-permute-done.4), channel_id=1, source_target_pairs={{0,7},{1,0},{2,1},{3,2},{4,3},{5,4},{6,5},{7,6},{8,15},{9,8},{10,9... | collective-permute-start | bytes 196616 | tf_op jit(solution)/shard_map/ppermute | solution.py:55
  19.4 5.2 %collective-permute-start.2 = (bf16[32,1024]{1,0:T(8,128)(2,1)S(1)}, bf16[32,1024]{1,0:T(8,128)(2,1)S(1)}, u32[]{:S(2)}, u32[]{:S(2)}) collective-permute-start(bf16[32,1024]{1,0:T(8,128)(2,1)S(1)} %collective-permute-done.1), channel_id=1, source_target_pairs={{0,1},{1,2},{2,3},{3,4},{4,5},{5,6},{6,7},{7,0},{8,9},{9,10},{10,1... | collective-permute-start | bytes 196616 | tf_op jit(solution)/shard_map/ppermute | solution.py:52
  20.2 10.0 %collective-permute-start.6 = (bf16[32,1024]{1,0:T(8,128)(2,1)S(1)}, bf16[32,1024]{1,0:T(8,128)(2,1)S(1)}, u32[]{:S(2)}, u32[]{:S(2)}) collective-permute-start(bf16[32,1024]{1,0:T(8,128)(2,1)S(1)} %collective-permute-done.5), channel_id=1, source_target_pairs={{0,7},{1,0},{2,1},{3,2},{4,3},{5,4},{6,5},{7,6},{8,15},{9,8},{10,9... | collective-permute-start | bytes 196616 | tf_op jit(solution)/shard_map/ppermute | solution.py:55
  24.6 5.5 %collective-permute-start.3 = (bf16[32,1024]{1,0:T(8,128)(2,1)S(1)}, bf16[32,1024]{1,0:T(8,128)(2,1)S(1)}, u32[]{:S(2)}, u32[]{:S(2)}) collective-permute-start(bf16[32,1024]{1,0:T(8,128)(2,1)S(1)} %collective-permute-done.2), channel_id=1, source_target_pairs={{0,1},{1,2},{2,3},{3,4},{4,5},{5,6},{6,7},{7,0},{8,9},{9,10},{10,1... | collective-permute-start | bytes 196616 | tf_op jit(solution)/shard_map/ppermute | solution.py:52
  30.9 12.7 %collective-permute-start.7 = (bf16[8,32,1024]{2,1,0:T(8,128)(2,1)S(1)}, bf16[8,32,1024]{2,1,0:T(8,128)(2,1)S(1)}, u32[]{:S(2)}, u32[]{:S(2)}) collective-permute-start(bf16[8,32,1024]{2,1,0:T(8,128)(2,1)S(1)} %broadcast_select_fusion.6), channel_id=1, source_target_pairs={{0,8},{1,9},{2,10},{3,11},{4,12},{5,13},{6,14},{7,15},{8,16},{9,17... | collective-permute-start | bytes 1572872 | tf_op jit(solution)/shard_map/ppermute | solution.py:52
  32.5 42.2 %copy-start.17 = (pred[48]{0:T(512)(128)(4,1)}, pred[48]{0:T(512)(128)(4,1)S(1)}, u32[]{:S(2)}) copy-start(pred[48]{0:T(512)(128)(4,1)S(1)} %compare_and_fusion.3) | copy-start | bytes 148
  32.5 12.4 %collective-permute-start.9 = (bf16[8,32,1024]{2,1,0:T(8,128)(2,1)S(1)}, bf16[8,32,1024]{2,1,0:T(8,128)(2,1)S(1)}, u32[]{:S(2)}, u32[]{:S(2)}) collective-permute-start(bf16[8,32,1024]{2,1,0:T(8,128)(2,1)S(1)} %broadcast_select_fusion.6), channel_id=1, source_target_pairs={{0,24},{1,25},{2,26},{3,27},{4,28},{5,29},{6,30},{7,31},{8,0},{9,1... | collective-permute-start | bytes 1572872 | tf_op jit(solution)/shard_map/ppermute | solution.py:55
  43.6 11.8 %collective-permute-start.8 = (bf16[8,32,1024]{2,1,0:T(8,128)(2,1)S(1)}, bf16[8,32,1024]{2,1,0:T(8,128)(2,1)S(1)}, u32[]{:S(2)}, u32[]{:S(2)}) collective-permute-start(bf16[8,32,1024]{2,1,0:T(8,128)(2,1)S(1)} %collective-permute-done.7), channel_id=1, source_target_pairs={{0,8},{1,9},{2,10},{3,11},{4,12},{5,13},{6,14},{7,15},{8,16},{9,17... | collective-permute-start | bytes 1572872 | tf_op jit(solution)/shard_map/ppermute | solution.py:52
  59.3 2.4 %copy-start.12 = (bf16[48,1024]{1,0:T(8,128)(2,1)S(1)}, bf16[48,1024]{1,0:T(8,128)(2,1)}, u32[]{:S(2)}) copy-start(bf16[48,1024]{1,0:T(8,128)(2,1)} %param.12) | copy-start | bytes 294916
  61.1 32.4 %collective-permute-start.10 = (bf16[1024,1024]{1,0:T(8,128)(2,1)}, bf16[1024,1024]{1,0:T(8,128)(2,1)}, u32[]{:S(2)}, u32[]{:S(2)}) collective-permute-start(bf16[1024,1024]{1,0:T(8,128)(2,1)} %bitcast_select_fusion), channel_id=1, source_target_pairs={{0,32},{32,0},{64,96},{96,64},{128,160},{160,128},{192,224},{224,1... | collective-permute-start | bytes 6291464 | tf_op jit(solution)/shard_map/ppermute | solution.py:105
  63.8 18.7 %all-to-all-start = ((f32[32,1,512]{2,1,0:T(1,128)}), f32[32,1,512]{2,1,0:T(1,128)S(1)}, u32[]{:S(2)}, u32[]{:S(2)}) async-start(f32[32,1,512]{2,1,0:T(1,128)} %reshape.269), calls=%async_computation | async-start | bytes 131072 | tf_op jit(solution)/shard_map/all_to_all | solution.py:100
  74.7 3.8 %copy-start.8 = (bf16[48,4,16]{2,1,0:T(4,128)(2,1)}, bf16[48,4,16]{2,1,0:T(4,128)(2,1)S(1)}, u32[]{:S(2)}) copy-start(bf16[48,4,16]{2,1,0:T(4,128)(2,1)S(1)} %gather_fusion) | copy-start | bytes 18436
  84.2 6.6 %copy-start.1 = (bf16[48,16,1024]{2,1,0:T(8,128)(2,1)S(1)}, bf16[48,16,1024]{2,1,0:T(8,128)(2,1)}, u32[]{:S(2)}) copy-start(bf16[48,16,1024]{2,1,0:T(8,128)(2,1)} %get-tuple-element.13) | copy-start | bytes 4718596
  89.2 4.3 %copy-start.10 = (f32[16,48,16]{1,0,2:T(8,128)}, f32[16,48,16]{1,0,2:T(8,128)S(1)}, u32[]{:S(2)}) copy-start(f32[16,48,16]{1,0,2:T(8,128)S(1)} %get-tuple-element.18) | copy-start | bytes 147460
  89.2 4.3 %copy-start.20 = (bf16[16,1024]{1,0:T(8,128)(2,1)S(1)}, bf16[16,1024]{1,0:T(8,128)(2,1)}, u32[]{:S(2)}) copy-start(bf16[16,1024]{1,0:T(8,128)(2,1)} %param.17) | copy-start | bytes 98308
  89.4 0.7 copy-start.13
  99.1 2.6 %copy-start.2 = (bf16[48,16,1024]{2,1,0:T(8,128)(2,1)S(1)}, bf16[48,16,1024]{2,1,0:T(8,128)(2,1)}, u32[]{:S(2)}) copy-start(bf16[48,16,1024]{2,1,0:T(8,128)(2,1)} %get-tuple-element.13) | copy-start | bytes 4718596
  101.7 1.2 copy-start.11
  101.7 1.2 copy-start.14
  101.7 4.2 %copy-start.7 = (bf16[48,1024]{1,0:T(8,128)(2,1)S(1)}, bf16[48,1024]{1,0:T(8,128)(2,1)}, u32[]{:S(2)}) copy-start(bf16[48,1024]{1,0:T(8,128)(2,1)} %pad_maximum_fusion.2) | copy-start | bytes 294916
  106.1 1.9 %copy-start.3 = (f32[48,16,1024]{2,1,0:T(8,128)S(1)}, f32[48,16,1024]{2,1,0:T(8,128)}, u32[]{:S(2)}) copy-start(f32[48,16,1024]{2,1,0:T(8,128)} %get-tuple-element.12) | copy-start | bytes 9437188
  106.1 1.9 %copy-start.9 = (bf16[48,4,16]{2,1,0:T(4,128)(2,1)S(1)}, bf16[48,4,16]{2,1,0:T(4,128)(2,1)}, u32[]{:S(2)}) copy-start(bf16[48,4,16]{2,1,0:T(4,128)(2,1)} %copy-done.8) | copy-start | bytes 18436
  106.1 1.9 %copy-start.18 = (pred[48]{0:T(512)(128)(4,1)S(1)}, pred[48]{0:T(512)(128)(4,1)}, u32[]{:S(2)}) copy-start(pred[48]{0:T(512)(128)(4,1)} %copy-done.17) | copy-start | bytes 148
  112.5 1.5 copy-start.15
  112.5 1.5 copy-start.16
  114.0 5.5 %copy-start.4 = (bf16[16,16,1024]{2,1,0:T(8,128)(2,1)S(1)}, bf16[16,16,1024]{2,1,0:T(8,128)(2,1)}, u32[]{:S(2)}) copy-start(bf16[16,16,1024]{2,1,0:T(8,128)(2,1)} %get-tuple-element.10) | copy-start | bytes 1572868
  114.1 5.5 %copy-start.5 = (bf16[16,16,1024]{2,1,0:T(8,128)(2,1)S(1)}, bf16[16,16,1024]{2,1,0:T(8,128)(2,1)}, u32[]{:S(2)}) copy-start(bf16[16,16,1024]{2,1,0:T(8,128)(2,1)} %get-tuple-element.11) | copy-start | bytes 1572868
  115.3 21.6 %all-to-all-start.2 = ((f32[8,9,32,128]{3,2,1,0:T(8,128)}), f32[8,9,32,128]{3,2,1,0:T(8,128)}, u32[]{:S(2)}, u32[]{:S(2)}) async-start(f32[8,9,32,128]{3,2,1,0:T(8,128)} %select_select_fusion), calls=%async_computation.2 | async-start | bytes 2359296 | tf_op jit(solution)/shard_map/all_to_all | solution.py:164
  122.5 3.0 %copy-start.6 = (bf16[32,16,1024]{2,1,0:T(8,128)(2,1)S(1)}, bf16[32,16,1024]{2,1,0:T(8,128)(2,1)}, u32[]{:S(2)}) copy-start(bf16[32,16,1024]{2,1,0:T(8,128)(2,1)} %pad_maximum_fusion.1) | copy-start | bytes 3145732
  139.1 17.8 %all-to-all-start.3 = ((f32[32,9,128]{2,1,0:T(8,128)}), f32[32,9,128]{2,1,0:T(8,128)S(1)}, u32[]{:S(2)}, u32[]{:S(2)}) async-start(f32[32,9,128]{2,1,0:T(8,128)} %copy.71), calls=%async_computation.3 | async-start | bytes 524288 | tf_op jit(solution)/shard_map/all_to_all | solution.py:165
